TPU v7x, 32 devices: a whole 2x2x4 slice. The times are simulated.
32 devices in a mesh: beam: 2 (over x), chan: 4 (over y, core), tm: 4 (over z).
Axes of the slice: x: 2, y: 2, z: 4, core: 2. Of those that a mesh axis runs over, the one named last changes fastest.
Arguments:
- samples: float32 [1024, 4096], P(('beam', 'chan'), 'tm'), parts along dimension 0, may hold values from -400 to 400, as said below
- offsets: int32 [9, 512], P(None, 'chan'), may hold values from 0 to 63, as said below
- template_weight: float32 [4, 128], replicated, may hold values from -0.5 to 0.5
- template_taps: int32 [4, 128], replicated, may hold values from 0 to 127, as said below
Outputs:
- matched: float32 [1024, 4, 4096], P(('beam', 'chan'), None, 'tm'), parts along dimension 0
There are 2 independent parts, one for each index of `beam`. A program takes and returns all parts, laid end to end along the dimension named above; an argument that names none is the same for every part. Nothing has to cross between parts.
Inputs may be any that keep to these rules, and one draw needn't show every extreme that they name: samples are finite floats; channel levels and spreads differ. offsets[l, g] is at most min(2^(l + 1), 64) - 1, and reaches that value for some g in every level l. `template_taps`: every template has a tap with lag 128 - 1; lags may repeat.
All inputs are finite; a program needn't handle non-finite values.
Results may differ from a plain program's by a relative error of at most 0.000098.
Values sent between devices are 32-bit elements; how exact they have to be, the bound alone decides.
No kernel may reach another device: no remote copies, remote signals or barrier semaphores. Data moves between devices by JAX's collectives and lax.ppermute only.
A program may use at most 64 MiB of HBM per device.

v0:
```python
import math

import jax
import jax.numpy as jnp
from jax import lax
from jax.sharding import PartitionSpec as P

SHIFT_CAP = 64


epsilon = 1e-05


def from_behind(value, axis, steps):
    count = lax.axis_size(axis)
    leading, last = (max(0, -steps), min(count, count - steps))
    return lax.ppermute(value, axis, [(source, source + steps) for source in range(leading, last)])


def swapped(block, axis, distance):
    count = lax.axis_size(axis)
    route = []
    for low in range(count):
        high = low | 1 << distance
        if high != low and high < count:
            route += [(low, high), (high, low)]
    return lax.ppermute(block, axis, route)


def shift_rows(upper_rows, offsets, window):
    current = upper_rows
    stride = 1
    while stride < window:
        chosen = offsets // stride % 2 == 1
        length = current.shape[1] - stride
        current = jnp.where(chosen[:, None], current[:, stride:], current[:, :length])
        stride = stride * 2
    return current


def local_level(spectra, level_offsets, row_count, window):
    row_total, length = spectra.shape
    groups = spectra.reshape(row_total // (2 * row_count), 2, row_count, length)
    lower_half = groups[:, 0]
    upper_half = groups[:, 1]
    lower_half = lower_half[:, :, : length - window + 1]
    lower_rows = jnp.concatenate([lower_half, lower_half], axis=1).reshape(row_total, -1)
    upper_rows = jnp.concatenate([upper_half, upper_half], axis=1).reshape(row_total, -1)
    return lower_rows + shift_rows(upper_rows, level_offsets, window)


def cross_level(spectra, level_offsets, window, bit_index):
    partner = swapped(spectra, "chan", bit_index)
    is_upper = lax.axis_index("chan") // 2**bit_index % 2 == 1
    lower_rows = jnp.where(is_upper, partner, spectra)
    upper_rows = jnp.where(is_upper, spectra, partner)
    lower_rows = lower_rows[:, : spectra.shape[1] - window + 1]
    return lower_rows + shift_rows(upper_rows, level_offsets, window)


def run_tree(spectra, offsets):
    chan_rows = spectra.shape[0]
    local_count = chan_rows.bit_length() - 1
    cross_count = lax.axis_size("chan").bit_length() - 1
    row_count = 1
    for level_index in range(local_count):
        window = min(2 ** (level_index + 1), SHIFT_CAP)
        spectra = local_level(spectra, offsets[level_index], row_count, window)
        row_count = row_count * 2
    for bit_index in range(cross_count):
        level_index = local_count + bit_index
        window = min(2 ** (level_index + 1), SHIFT_CAP)
        spectra = cross_level(spectra, offsets[level_index], window, bit_index)
    return spectra


def lag_weights(template_weight, template_taps):
    tap_count = template_weight.shape[1]
    onehot = (
        template_taps[:, :, None] == jnp.arange(tap_count, dtype=jnp.int32)[None, None, :]
    ).astype(jnp.float32)
    return jnp.einsum("mk,mkl->ml", template_weight, onehot, precision=lax.Precision.HIGHEST)


def toeplitz_band(pattern, block_len):
    templ_count, period = pattern.shape
    tiled = jnp.tile(pattern, (1, block_len))[:, : block_len * (period - 1)]
    rows_view = tiled.reshape(templ_count, block_len, period - 1)[:, :, :block_len]
    return jnp.swapaxes(rows_view, 1, 2)


def make_bands(lag_weight):
    templ_count, tap_count = lag_weight.shape
    block_len = 2 * tap_count
    spare = jnp.zeros((templ_count, block_len - tap_count), jnp.float32)
    empty = jnp.zeros((templ_count, block_len), jnp.float32)
    pattern_now = jnp.concatenate([lag_weight, spare, empty], axis=1)
    pattern_next = jnp.concatenate([empty, lag_weight, spare], axis=1)
    return (toeplitz_band(pattern_now, block_len), toeplitz_band(pattern_next, block_len))


def filter_blocks(padded_rows, lag_weight):
    band_now, band_next = make_bands(lag_weight)
    row_total, length = padded_rows.shape
    block_len = band_now.shape[1]
    blocks = padded_rows.reshape(row_total, length // block_len, block_len)
    result = jnp.einsum("rni,mit->rmnt", blocks[:, :-1], band_now, precision=lax.Precision.HIGHEST)
    result = result + jnp.einsum(
        "rni,mit->rmnt", blocks[:, 1:], band_next, precision=lax.Precision.HIGHEST
    )
    return result.reshape(row_total, band_now.shape[0], -1)


def shards(samples, offsets, template_weight, template_taps):
    chan_rows, time_length = samples.shape
    chan_count = lax.axis_size("chan")
    sample_total = time_length * lax.axis_size("tm")
    totals, squares = lax.psum((jnp.sum(samples, axis=1), jnp.sum(samples * samples, axis=1)), "tm")
    average = totals[:, None] / sample_total
    mean_square = squares[:, None] / sample_total
    scaling = lax.rsqrt(mean_square - average * average + epsilon) / math.sqrt(
        chan_rows * chan_count
    )
    spectra = (samples - average) * scaling
    level_total = (chan_rows * chan_count).bit_length() - 1
    tree_margin = sum(
        (min(2 ** (level_index + 1), SHIFT_CAP) - 1 for level_index in range(level_total))
    )
    filter_margin = template_taps.shape[1] - 1
    edge_samples = from_behind(spectra[:, : tree_margin + filter_margin], "tm", -1)
    spectra = run_tree(jnp.concatenate([spectra, edge_samples], axis=1), offsets)
    lag_weight = lag_weights(template_weight, template_taps)
    block_len = 2 * template_taps.shape[1]
    padded = jnp.concatenate(
        [spectra, jnp.zeros((chan_rows, block_len - filter_margin), jnp.float32)], axis=1
    )
    return filter_blocks(padded, lag_weight)


def solution(mesh):
    in_specs = (P(("beam", "chan"), "tm"), P(None, "chan"), P(), P())
    out_specs = P(("beam", "chan"), None, "tm")
    return jax.shard_map(shards, mesh=mesh, in_specs=in_specs, out_specs=out_specs, check_vma=False)
```

profile of v0, /device:TPU:0, one launch (start us, length us, event | category | flops | bytes accessed | tf_op | source)
XLA Modules:
  0.0 69.6 jit_solution(7379995091926438821)
XLA Ops:
  0.0 1.2 %fusion.88 = (f32[128]{0:T(128)S(1)}, f32[128]{0:T(128)S(1)}) fusion(f32[128,1024]{1,0:T(8,128)} %param.4), kind=kLoop, calls=%fused_computation.388 | loop fusion | flops 392960 | bytes 525312 | tf_op jit(solution)/shard_map/reduce_sum | solution.py:118
  1.2 13.5 %all-reduce.1 = (f32[128]{0:T(128)S(1)}, f32[128]{0:T(128)S(1)}) all-reduce(f32[128]{0:T(128)S(1)} %get-tuple-element.6, f32[128]{0:T(128)S(1)} %get-tuple-element.5), channel_id=1, replica_groups=mesh['beam'=2,'chan'=4,'tm'=4] {'tm'}, use_global_device_ids=true, to_apply=%region_3.0 | all-reduce | flops 256 | bytes 2048 | tf_op jit(solution)/shard_map/psum | solution.py:118
  14.7 1.2 %subtract_multiply_fusion = f32[128,1024]{1,0:T(8,128)S(1)} fusion(f32[128,1024]{1,0:T(8,128)} %param.4, f32[128]{0:T(128)S(1)} %get-tuple-element.69, f32[128]{0:T(128)S(1)} %get-tuple-element.68), kind=kLoop, calls=%fused_computation.74 | loop fusion | flops 262144 | bytes 1049600 | tf_op jit(solution)/shard_map/mul | solution.py:124
  15.9 1.3 %collective-permute-start = (f32[128,436]{1,0:T(8,128)S(1)}, f32[128,436]{1,0:T(8,128)S(1)}, u32[]{:S(2)}, u32[]{:S(2)}) collective-permute-start(f32[128,436]{1,0:T(8,128)S(1)} %slice.470), channel_id=1, source_target_pairs={{1,0},{2,1},{3,2},{5,4},{6,5},{7,6},{9,8},{10,9},{11,10},{13,12},{... | collective-permute-start | bytes 669704 | tf_op jit(solution)/shard_map/ppermute | solution.py:17
  17.4 6.8 %collective-permute-done = f32[128,436]{1,0:T(8,128)S(1)} collective-permute-done((f32[128,436]{1,0:T(8,128)S(1)}, f32[128,436]{1,0:T(8,128)S(1)}, u32[]{:S(2)}, u32[]{:S(2)}) %collective-permute-start) | collective-permute-done | bytes 223264 | tf_op jit(solution)/shard_map/ppermute | solution.py:17
  24.2 0.5 reshape.1294
  24.7 0.6 slice_bitcast_fusion.16
  25.3 0.6 pad_maximum_fusion.1
  25.9 0.5 reshape.1295
  26.5 0.6 pad_maximum_fusion.2
  27.1 0.5 reshape.1296
  27.6 0.3 fusion.4
  27.9 0.5 reshape.1297
  28.5 0.3 pad_maximum_fusion.3
  28.8 0.3 reshape.1298
  29.1 0.3 pad_maximum_fusion.4
  29.4 0.3 reshape.1299
  29.7 0.3 slice_select_fusion.12
  30.0 0.3 fusion.3
  30.7 0.3 slice_select_fusion.10
  31.0 0.3 slice_select_fusion.9
  31.3 0.3 fusion.2
  31.8 0.3 slice_select_fusion.7
  32.1 0.3 slice_select_fusion.6
  32.4 0.3 slice_select_fusion.5
  32.7 0.3 fusion.1
  33.2 0.3 slice_select_fusion.3
  33.5 0.3 slice_select_fusion.2
  33.8 0.3 slice_select_fusion.1
  34.1 0.3 slice_select_fusion
  36.9 0.4 slice_select_fusion.17
  38.5 2.0 %collective-permute-done.1 = f32[128,1277]{1,0:T(8,128)S(1)} collective-permute-done((f32[128,1277]{1,0:T(8,128)S(1)}, f32[128,1277]{1,0:T(8,128)S(1)}, u32[]{:S(2)}, u32[]{:S(2)}) %collective-permute-start.1) | collective-permute-done | bytes 653856 | tf_op jit(solution)/shard_map/ppermute | solution.py:27
  41.9 0.3 fusion.7
  42.2 1.1 %copy.25 = f32[128,1214]{0,1:T(8,128)} copy(f32[128,1214]{1,0:T(8,128)S(1)} %fusion.7) | data formatting | bytes 1243136 | tf_op jit(solution)/shard_map/add | solution.py:58
  43.3 1.5 %collective-permute-start.2 = (f32[128,1214]{0,1:T(8,128)}, f32[128,1214]{0,1:T(8,128)S(1)}, u32[]{:S(2)}, u32[]{:S(2)}) collective-permute-start(f32[128,1214]{0,1:T(8,128)} %copy.25), channel_id=1, source_target_pairs={{0,8},{8,0},{4,12},{12,4},{1,9},{9,1},{5,13},{13,5},{2,10},{10,2},... | collective-permute-start | bytes 1864712 | tf_op jit(solution)/shard_map/ppermute | solution.py:27
  44.8 0.3 fusion.10
  45.2 0.4 broadcast_bitcast_fusion
  45.6 1.4 %copy.42 = f32[1,4,256,512]{3,1,2,0:T(4,128)S(1)} copy(f32[1,4,256,512]{3,2,1,0:T(8,128)S(1)} %get-tuple-element.70) | data formatting | bytes 4194304
  46.9 1.4 %slice.575 = f32[4,130816]{1,0:T(4,128)} slice(f32[4,131072]{1,0:T(4,128)S(1)} %bitcast.363), slice={[0:4], [0:130816]} | slice | bytes 4186112 | tf_op jit(solution)/shard_map/slice | solution.py:87
  48.4 5.1 %reshape.1316 = f32[4,256,511]{2,1,0:T(8,128)} reshape(f32[4,130816]{1,0:T(4,128)} %slice.575) | data formatting | bytes 4186112 | tf_op jit(solution)/shard_map/reshape | solution.py:88
  53.5 1.4 %copy.41 = f32[1,4,256,512]{3,1,2,0:T(4,128)S(1)} copy(f32[1,4,256,512]{3,2,1,0:T(8,128)S(1)} %get-tuple-element.71) | data formatting | bytes 4194304
  55.0 3.6 %reshape.1293 = f32[4,256,511]{2,1,0:T(8,128)} reshape(f32[4,130816]{1,0:T(4,128)S(1)} %slice.468) | data formatting | bytes 4186112 | tf_op jit(solution)/shard_map/reshape | solution.py:88
  58.6 1.0 %collective-permute-done.2 = f32[128,1214]{0,1:T(8,128)S(1)} collective-permute-done((f32[128,1214]{0,1:T(8,128)}, f32[128,1214]{0,1:T(8,128)S(1)}, u32[]{:S(2)}, u32[]{:S(2)}) %collective-permute-start.2) | collective-permute-done | bytes 621600 | tf_op jit(solution)/shard_map/ppermute | solution.py:27
  61.2 1.1 %fusion.9 = f32[128,1151]{1,0:T(8,128)} fusion(f32[128,1183]{1,0:T(8,128)S(1)} %slice_select_fusion.26, f32[128,1214]{1,0:T(8,128)S(1)} %fusion.7, f32[128,1214]{1,0:T(8,128)S(1)} %copy.26, pred[128]{0:T(512)(128)(4,1)S(1)} %get-tuple-element.29, pred[]{:T(512)S(6)} %eq.338), kind=kLoop, calls=%fused_computation.69 | loop fusion | flops 441984 | bytes 2946689 | tf_op jit(solution)/shard_map/add | solution.py:58
  62.3 1.3 %copy.40 = f32[128,1151]{0,1:T(8,128)S(1)} copy(f32[128,1151]{1,0:T(8,128)} %fusion.9) | data formatting | bytes 1178624
  63.9 1.8 %fusion = f32[4,256,128,4]{2,1,3,0:T(8,128)S(1)} fusion(f32[4,256,511]{2,1,0:T(8,128)S(1)} %copy-done.1, f32[128,5,256]{0,2,1:T(8,128)S(1)} %bitcast.368), kind=kOutput, calls=%fused_computation.3 | convolution fusion | flops 1610612736 | bytes 3670016 | tf_op jit(solution)/shard_map/rni,mit->rmnt/dot_general | solution.py:107
  65.7 1.9 %convolution_add_fusion = f32[4,256,128,4]{2,1,3,0:T(8,128)S(1)} fusion(f32[4,256,128,4]{2,1,3,0:T(8,128)S(1)} %fusion, f32[4,256,511]{2,1,0:T(8,128)S(1)} %copy-done.2, f32[128,5,256]{0,2,1:T(8,128)S(1)} %bitcast.369), kind=kOutput, calls=%fused_computation | convolution fusion | flops 1611137024 | bytes 5767168 | tf_op jit(solution)/shard_map/rni,mit->rmnt/dot_general | solution.py:108
  67.6 2.0 %copy.31 = f32[128,4,1024]{2,1,0:T(4,128)} copy(f32[128,4,1024]{0,2,1:T(8,128)S(1)} %bitcast.362) | data formatting | bytes 4194304 | tf_op jit(solution)/shard_map/reshape | solution.py:111
  (65 shorter events, 8.0 us)
Async XLA Ops:
  0.0 44.8 %copy-start = (f32[4,128]{1,0:T(4,128)S(1)}, f32[4,128]{1,0:T(4,128)}, u32[]{:S(2)}) copy-start(f32[4,128]{1,0:T(4,128)} %param.6) | copy-start | bytes 6148
  0.0 17.2 %copy-start.3 = (s32[9,128]{1,0:T(8,128)S(1)}, s32[9,128]{1,0:T(8,128)}, u32[]{:S(2)}) copy-start(s32[9,128]{1,0:T(8,128)} %param.5) | copy-start | bytes 13828
  15.9 8.3 %collective-permute-start = (f32[128,436]{1,0:T(8,128)S(1)}, f32[128,436]{1,0:T(8,128)S(1)}, u32[]{:S(2)}, u32[]{:S(2)}) collective-permute-start(f32[128,436]{1,0:T(8,128)S(1)} %slice.470), channel_id=1, source_target_pairs={{1,0},{2,1},{3,2},{5,4},{6,5},{7,6},{9,8},{10,9},{11,10},{13,12},{... | collective-permute-start | bytes 669704 | tf_op jit(solution)/shard_map/ppermute | solution.py:17
  38.4 2.2 %collective-permute-start.1 = (f32[128,1277]{1,0:T(8,128)S(1)}, f32[128,1277]{1,0:T(8,128)S(1)}, u32[]{:S(2)}, u32[]{:S(2)}) collective-permute-start(f32[128,1277]{1,0:T(8,128)S(1)} %fusion.8), channel_id=1, source_target_pairs={{0,4},{4,0},{8,12},{12,8},{1,5},{5,1},{9,13},{13,9},{2,6},{6,2},{1... | collective-permute-start | bytes 1961480 | tf_op jit(solution)/shard_map/ppermute | solution.py:27
  41.9 2.9 %copy-start.4 = (s32[4,128]{1,0:T(4,128)S(1)}, s32[4,128]{1,0:T(4,128)}, u32[]{:S(2)}) copy-start(s32[4,128]{1,0:T(4,128)} %param.7) | copy-start | bytes 6148
  43.3 16.3 %collective-permute-start.2 = (f32[128,1214]{0,1:T(8,128)}, f32[128,1214]{0,1:T(8,128)S(1)}, u32[]{:S(2)}, u32[]{:S(2)}) collective-permute-start(f32[128,1214]{0,1:T(8,128)} %copy.25), channel_id=1, source_target_pairs={{0,8},{8,0},{4,12},{12,4},{1,9},{9,1},{5,13},{13,5},{2,10},{10,2},... | collective-permute-start | bytes 1864712 | tf_op jit(solution)/shard_map/ppermute | solution.py:27
  61.2 2.7 %copy-start.1 = (f32[4,256,511]{2,1,0:T(8,128)S(1)}, f32[4,256,511]{2,1,0:T(8,128)}, u32[]{:S(2)}) copy-start(f32[4,256,511]{2,1,0:T(8,128)} %reshape.1293) | copy-start | bytes 6279172
  63.9 1.8 %copy-start.2 = (f32[4,256,511]{2,1,0:T(8,128)S(1)}, f32[4,256,511]{2,1,0:T(8,128)}, u32[]{:S(2)}) copy-start(f32[4,256,511]{2,1,0:T(8,128)} %reshape.1316) | copy-start | bytes 6279172
where the time goes:
time: 69.8 us; the launch traced here: 69.6 us
  local copies, waits for them, and re-layouts  22.1 us (32%)
  other arithmetic  16.7 us (24%)
  blocking collectives  13.5 us (19%)
  waiting for transfers between devices  9.79 us (14%)
  matrix products  4.02 us (6%)
  starting transfers between devices  2.88 us (4%)
    psum x1, blocking collectives, shards(): lax.psum((jnp.sum(samples, axis=1), jnp.sum(samples * samples, axis=1)),...  13.5 us
    reshape x2, local copies, waits for them, and re-layouts, toeplitz_band(): tiled.reshape(templ_count, block_len, period - 1)[:, :, :block_len]  8.75 us
    select_n x30, other arithmetic, shift_rows(): jnp.where(chosen[:, None], current[:, stride:], current[:, :length])  8.25 us
    ppermute x1, waiting for transfers between devices, from_behind(): lax.ppermute(value, axis, [(source, source + steps) for source in range(l...  6.76 us
    unnamed x14, local copies, waits for them, and re-layouts  4.4 us
    ppermute x2, waiting for transfers between devices, swapped(): return lax.ppermute(block, axis, route)  3.03 us
    add x7, other arithmetic, local_level(): return lower_rows + shift_rows(upper_rows, level_offsets, window)  1.97 us
    reshape x1, local copies, waits for them, and re-layouts, filter_blocks(): return result.reshape(row_total, band_now.shape[0], -1)  1.97 us
  transfers between devices with their start and end apart: 3, of which 3 were waited for; matrix products, arithmetic and copies ran while one was open for 20% of the time, Pallas kernels for 0%

commit v1 on v0

--- a/solution.py
+++ b/solution.py
@@ -25,6 +25,17 @@
         if high != low and high < count:
             route += [(low, high), (high, low)]
     return lax.ppermute(block, axis, route)
+
+
+def butterfly_sum(value, axis):
+    count = lax.axis_size(axis)
+    if count & (count - 1):
+        return lax.psum(value, axis)
+    distance = 0
+    while 1 << distance < count:
+        value = value + swapped(value, axis, distance)
+        distance = distance + 1
+    return value
 
 
 def shift_rows(upper_rows, offsets, window):
@@ -115,7 +126,9 @@
     chan_rows, time_length = samples.shape
     chan_count = lax.axis_size("chan")
     sample_total = time_length * lax.axis_size("tm")
-    totals, squares = lax.psum((jnp.sum(samples, axis=1), jnp.sum(samples * samples, axis=1)), "tm")
+    totals, squares = butterfly_sum(
+        jnp.stack([jnp.sum(samples, axis=1), jnp.sum(samples * samples, axis=1)]), "tm"
+    )
     average = totals[:, None] / sample_total
     mean_square = squares[:, None] / sample_total
     scaling = lax.rsqrt(mean_square - average * average + epsilon) / math.sqrt(

time: 69.8 us -> 66.3 us (0.950)
  blocking collectives: 13.5 us -> 0 us
  starting transfers between devices: 2.88 us -> 8.71 us
  waiting for transfers between devices: 9.79 us -> 12 us
  other arithmetic: 16.7 us -> 18.4 us
    psum x1 -> x0, blocking collectives: 13.5 us -> none  [shards(): lax.psum((jnp.sum(samples, axis=1), jnp.sum(samples * samples, axis=1)),...]
    ppermute x2 -> x4, starting transfers between devices: 1.59 us -> 7.42 us  [swapped(): return lax.ppermute(block, axis, route)]
    ppermute x2 -> x4, waiting for transfers between devices: 3.03 us -> 4.84 us  [swapped(): return lax.ppermute(block, axis, route)]
    eq x4, other arithmetic: 0.17 us -> 1.94 us  [shift_rows(): chosen = offsets // stride % 2 == 1]
    unnamed x14 -> x12, local copies, waits for them, and re-layouts: 4.4 us -> 4.39 us
  transfers between devices with their start and end apart: 3 -> 5, of which waited for: 3 -> 4; matrix products, arithmetic and copies ran while one was open for 20% -> 24% of each run, Pallas kernels for 0% -> 0%
where the time goes in v1:
time: 66.3 us; the launch traced here: 66 us
  local copies, waits for them, and re-layouts  21.9 us (33%)
  other arithmetic  18.4 us (28%)
  waiting for transfers between devices  12 us (18%)
  starting transfers between devices  8.71 us (13%)
  matrix products  4.26 us (6%)
    reshape x2, local copies, waits for them, and re-layouts, toeplitz_band(): tiled.reshape(templ_count, block_len, period - 1)[:, :, :block_len]  8.76 us
    select_n x30, other arithmetic, shift_rows(): jnp.where(chosen[:, None], current[:, stride:], current[:, :length])  8.24 us
    ppermute x4, starting transfers between devices, swapped(): return lax.ppermute(block, axis, route)  7.42 us
    ppermute x1, waiting for transfers between devices, from_behind(): lax.ppermute(value, axis, [(source, source + steps) for source in range(l...  7.2 us
    ppermute x4, waiting for transfers between devices, swapped(): return lax.ppermute(block, axis, route)  4.84 us
    unnamed x12, local copies, waits for them, and re-layouts  4.39 us
    dot_general x1, matrix products, filter_blocks(): jnp.einsum('rni,mit->rmnt', blocks[:, :-1], band_now, precision=lax.Preci...  2.06 us
    reshape x1, local copies, waits for them, and re-layouts, filter_blocks(): return result.reshape(row_total, band_now.shape[0], -1)  1.97 us
  transfers between devices with their start and end apart: 5, of which 4 were waited for; matrix products, arithmetic and copies ran while one was open for 24% of the time, Pallas kernels for 0%

profile of v1, /device:TPU:0, one launch (start us, length us, event | category | flops | bytes accessed | tf_op | source)
XLA Modules:
  0.0 66.0 jit_solution(5440932274638204007)
XLA Ops:
  0.0 1.2 %fusion.92 = (f32[128]{0:T(128)S(1)}, f32[128]{0:T(128)S(1)}) fusion(f32[128,1024]{1,0:T(8,128)} %param.4), kind=kLoop, calls=%fused_computation.393 | loop fusion | flops 392960 | bytes 525312 | tf_op jit(solution)/shard_map/reduce_sum | solution.py:130
  1.2 3.1 %collective-permute-start = (f32[2,128]{1,0:T(2,128)S(1)}, f32[2,128]{1,0:T(2,128)S(1)}, u32[]{:S(2)}, u32[]{:S(2)}) collective-permute-start(f32[2,128]{1,0:T(2,128)S(1)} %pad_maximum_fusion.13), channel_id=1, source_target_pairs={{0,1},{1,0},{2,3},{3,2},{4,5},{5,4},{6,7},{7,6},{8,9},{9,8},{10,11... | collective-permute-start | bytes 3080 | tf_op jit(solution)/shard_map/ppermute | solution.py:27
  4.3 0.9 %fusion.45 = (pred[128]{0:T(512)(128)(4,1)S(1)}, pred[128]{0:T(512)(128)(4,1)S(1)}, pred[128]{0:T(512)(128)(4,1)S(1)}, pred[128]{0:T(512)(128)(4,1)S(1)}, pred[1...) fusion(s32[9,128]{1,0:T(8,128)} %param.5), kind=kLoop, calls=%fused_computation.329 | loop fusion | flops 51328 | bytes 6016 | tf_op jit(solution)/shard_map/eq | solution.py:45
  5.3 1.0 %fusion.46 = (pred[128]{0:T(512)(128)(4,1)S(1)}, pred[128]{0:T(512)(128)(4,1)S(1)}, pred[128]{0:T(512)(128)(4,1)S(1)}, pred[128]{0:T(512)(128)(4,1)S(1)}, pred[1...) fusion(s32[9,128]{1,0:T(8,128)} %param.5), kind=kLoop, calls=%fused_computation.330 | loop fusion | flops 46720 | bytes 6400 | tf_op jit(solution)/shard_map/eq | solution.py:45
  6.3 2.7 %collective-permute-start.1 = (f32[2,128]{1,0:T(2,128)S(1)}, f32[2,128]{1,0:T(2,128)S(1)}, u32[]{:S(2)}, u32[]{:S(2)}) collective-permute-start(f32[2,128]{1,0:T(2,128)S(1)} %fusion.91), channel_id=1, source_target_pairs={{0,2},{2,0},{1,3},{3,1},{4,6},{6,4},{5,7},{7,5},{8,10},{10,8},{9,1... | collective-permute-start | bytes 3080 | tf_op jit(solution)/shard_map/ppermute | solution.py:27
  9.0 1.8 %collective-permute-done.1 = f32[2,128]{1,0:T(2,128)S(1)} collective-permute-done((f32[2,128]{1,0:T(2,128)S(1)}, f32[2,128]{1,0:T(2,128)S(1)}, u32[]{:S(2)}, u32[]{:S(2)}) %collective-permute-start.1) | collective-permute-done | bytes 1056 | tf_op jit(solution)/shard_map/ppermute | solution.py:27
  10.9 1.2 %subtract_multiply_fusion = f32[128,1024]{1,0:T(8,128)S(1)} fusion(f32[128,1024]{1,0:T(8,128)} %param.4, f32[128]{0:T(128)S(1)} %fusion.90, f32[128]{0:T(128)S(1)} %multiply_bitcast_fusion), kind=kLoop, calls=%fused_computation.73 | loop fusion | flops 262144 | bytes 1049600 | tf_op jit(solution)/shard_map/mul | solution.py:137
  12.1 1.3 %collective-permute-start.2 = (f32[128,436]{1,0:T(8,128)S(1)}, f32[128,436]{1,0:T(8,128)S(1)}, u32[]{:S(2)}, u32[]{:S(2)}) collective-permute-start(f32[128,436]{1,0:T(8,128)S(1)} %slice.470), channel_id=1, source_target_pairs={{1,0},{2,1},{3,2},{5,4},{6,5},{7,6},{9,8},{10,9},{11,10},{13,12},{... | collective-permute-start | bytes 669704 | tf_op jit(solution)/shard_map/ppermute | solution.py:17
  13.4 7.2 %collective-permute-done.2 = f32[128,436]{1,0:T(8,128)S(1)} collective-permute-done((f32[128,436]{1,0:T(8,128)S(1)}, f32[128,436]{1,0:T(8,128)S(1)}, u32[]{:S(2)}, u32[]{:S(2)}) %collective-permute-start.2) | collective-permute-done | bytes 223264 | tf_op jit(solution)/shard_map/ppermute | solution.py:17
  20.6 0.5 reshape.1316
  21.1 0.6 slice_bitcast_fusion.16
  21.7 0.6 pad_maximum_fusion.1
  22.3 0.5 reshape.1317
  22.9 0.6 pad_maximum_fusion.2
  23.5 0.5 reshape.1318
  24.0 0.3 fusion.4
  24.3 0.5 reshape.1319
  24.9 0.3 pad_maximum_fusion.3
  25.5 0.3 pad_maximum_fusion.4
  26.1 0.3 slice_select_fusion.12
  26.3 0.3 fusion.3
  27.1 0.3 slice_select_fusion.10
  27.4 0.3 slice_select_fusion.9
  27.7 0.3 fusion.2
  28.2 0.3 slice_select_fusion.7
  28.5 0.3 slice_select_fusion.6
  28.8 0.3 slice_select_fusion.5
  29.1 0.3 fusion.1
  29.6 0.3 slice_select_fusion.3
  29.9 0.3 slice_select_fusion.2
  30.5 0.3 slice_select_fusion
  33.6 0.4 slice_select_fusion.16
  34.9 2.0 %collective-permute-done.3 = f32[128,1277]{1,0:T(8,128)S(1)} collective-permute-done((f32[128,1277]{1,0:T(8,128)S(1)}, f32[128,1277]{1,0:T(8,128)S(1)}, u32[]{:S(2)}, u32[]{:S(2)}) %collective-permute-start.3) | collective-permute-done | bytes 653856 | tf_op jit(solution)/shard_map/ppermute | solution.py:27
  38.6 1.1 %copy.25 = f32[128,1214]{0,1:T(8,128)} copy(f32[128,1214]{1,0:T(8,128)S(1)} %fusion.7) | data formatting | bytes 1243136 | tf_op jit(solution)/shard_map/add | solution.py:69
  39.7 1.5 %collective-permute-start.4 = (f32[128,1214]{0,1:T(8,128)}, f32[128,1214]{0,1:T(8,128)S(1)}, u32[]{:S(2)}, u32[]{:S(2)}) collective-permute-start(f32[128,1214]{0,1:T(8,128)} %copy.25), channel_id=1, source_target_pairs={{0,8},{8,0},{4,12},{12,4},{1,9},{9,1},{5,13},{13,5},{2,10},{10,2},... | collective-permute-start | bytes 1864712 | tf_op jit(solution)/shard_map/ppermute | solution.py:27
  41.2 0.3 fusion.10
  41.5 0.4 broadcast_bitcast_fusion
  41.9 1.4 %copy.42 = f32[1,4,256,512]{3,1,2,0:T(4,128)S(1)} copy(f32[1,4,256,512]{3,2,1,0:T(8,128)S(1)} %get-tuple-element.66) | data formatting | bytes 4194304
  43.3 1.4 %slice.575 = f32[4,130816]{1,0:T(4,128)} slice(f32[4,131072]{1,0:T(4,128)S(1)} %bitcast.377), slice={[0:4], [0:130816]} | slice | bytes 4186112 | tf_op jit(solution)/shard_map/slice | solution.py:98
  44.7 5.1 %reshape.1338 = f32[4,256,511]{2,1,0:T(8,128)} reshape(f32[4,130816]{1,0:T(4,128)} %slice.575) | data formatting | bytes 4186112 | tf_op jit(solution)/shard_map/reshape | solution.py:99
  49.9 1.4 %copy.41 = f32[1,4,256,512]{3,1,2,0:T(4,128)S(1)} copy(f32[1,4,256,512]{3,2,1,0:T(8,128)S(1)} %get-tuple-element.67) | data formatting | bytes 4194304
  51.4 3.6 %reshape.1315 = f32[4,256,511]{2,1,0:T(8,128)} reshape(f32[4,130816]{1,0:T(4,128)S(1)} %slice.468) | data formatting | bytes 4186112 | tf_op jit(solution)/shard_map/reshape | solution.py:99
  55.0 1.0 %collective-permute-done.4 = f32[128,1214]{0,1:T(8,128)S(1)} collective-permute-done((f32[128,1214]{0,1:T(8,128)}, f32[128,1214]{0,1:T(8,128)S(1)}, u32[]{:S(2)}, u32[]{:S(2)}) %collective-permute-start.4) | collective-permute-done | bytes 621600 | tf_op jit(solution)/shard_map/ppermute | solution.py:27
  57.6 1.1 %fusion.9 = f32[128,1151]{1,0:T(8,128)} fusion(f32[128,1183]{1,0:T(8,128)S(1)} %slice_select_fusion.26, f32[128,1214]{1,0:T(8,128)S(1)} %fusion.7, f32[128,1214]{1,0:T(8,128)S(1)} %copy.26, pred[128]{0:T(512)(128)(4,1)S(1)} %get-tuple-element.27, pred[]{:T(512)S(6)} %eq.338), kind=kLoop, calls=%fused_computation.69 | loop fusion | flops 441984 | bytes 2946689 | tf_op jit(solution)/shard_map/add | solution.py:69
  58.6 1.3 %copy.40 = f32[128,1151]{0,1:T(8,128)S(1)} copy(f32[128,1151]{1,0:T(8,128)} %fusion.9) | data formatting | bytes 1178624
  60.0 2.1 %fusion = f32[4,256,128,4]{2,1,3,0:T(8,128)S(1)} fusion(f32[4,256,511]{2,1,0:T(8,128)S(1)} %copy-done.1, f32[128,5,256]{0,2,1:T(8,128)S(1)} %bitcast.382), kind=kOutput, calls=%fused_computation.3 | convolution fusion | flops 1610612736 | bytes 3670016 | tf_op jit(solution)/shard_map/rni,mit->rmnt/dot_general | solution.py:118
  62.1 1.9 %convolution_add_fusion = f32[4,256,128,4]{2,1,3,0:T(8,128)S(1)} fusion(f32[4,256,128,4]{2,1,3,0:T(8,128)S(1)} %fusion, f32[4,256,511]{2,1,0:T(8,128)S(1)} %copy-done.2, f32[128,5,256]{0,2,1:T(8,128)S(1)} %bitcast.383), kind=kOutput, calls=%fused_computation | convolution fusion | flops 1611137024 | bytes 5767168 | tf_op jit(solution)/shard_map/rni,mit->rmnt/dot_general | solution.py:119
  64.0 2.0 %copy.31 = f32[128,4,1024]{2,1,0:T(4,128)} copy(f32[128,4,1024]{0,2,1:T(8,128)S(1)} %bitcast.376) | data formatting | bytes 4194304 | tf_op jit(solution)/shard_map/reshape | solution.py:122
  (70 shorter events, 8.8 us)
Async XLA Ops:
  0.0 41.2 %copy-start = (f32[4,128]{1,0:T(4,128)S(1)}, f32[4,128]{1,0:T(4,128)}, u32[]{:S(2)}) copy-start(f32[4,128]{1,0:T(4,128)} %param.6) | copy-start | bytes 6148
  1.2 5.0 %collective-permute-start = (f32[2,128]{1,0:T(2,128)S(1)}, f32[2,128]{1,0:T(2,128)S(1)}, u32[]{:S(2)}, u32[]{:S(2)}) collective-permute-start(f32[2,128]{1,0:T(2,128)S(1)} %pad_maximum_fusion.13), channel_id=1, source_target_pairs={{0,1},{1,0},{2,3},{3,2},{4,5},{5,4},{6,7},{7,6},{8,9},{9,8},{10,11... | collective-permute-start | bytes 3080 | tf_op jit(solution)/shard_map/ppermute | solution.py:27
  6.3 4.5 %collective-permute-start.1 = (f32[2,128]{1,0:T(2,128)S(1)}, f32[2,128]{1,0:T(2,128)S(1)}, u32[]{:S(2)}, u32[]{:S(2)}) collective-permute-start(f32[2,128]{1,0:T(2,128)S(1)} %fusion.91), channel_id=1, source_target_pairs={{0,2},{2,0},{1,3},{3,1},{4,6},{6,4},{5,7},{7,5},{8,10},{10,8},{9,1... | collective-permute-start | bytes 3080 | tf_op jit(solution)/shard_map/ppermute | solution.py:27
  12.1 8.5 %collective-permute-start.2 = (f32[128,436]{1,0:T(8,128)S(1)}, f32[128,436]{1,0:T(8,128)S(1)}, u32[]{:S(2)}, u32[]{:S(2)}) collective-permute-start(f32[128,436]{1,0:T(8,128)S(1)} %slice.470), channel_id=1, source_target_pairs={{1,0},{2,1},{3,2},{5,4},{6,5},{7,6},{9,8},{10,9},{11,10},{13,12},{... | collective-permute-start | bytes 669704 | tf_op jit(solution)/shard_map/ppermute | solution.py:17
  34.8 2.2 %collective-permute-start.3 = (f32[128,1277]{1,0:T(8,128)S(1)}, f32[128,1277]{1,0:T(8,128)S(1)}, u32[]{:S(2)}, u32[]{:S(2)}) collective-permute-start(f32[128,1277]{1,0:T(8,128)S(1)} %fusion.8), channel_id=1, source_target_pairs={{0,4},{4,0},{8,12},{12,8},{1,5},{5,1},{9,13},{13,9},{2,6},{6,2},{1... | collective-permute-start | bytes 1961480 | tf_op jit(solution)/shard_map/ppermute | solution.py:27
  38.3 2.9 %copy-start.3 = (s32[4,128]{1,0:T(4,128)S(1)}, s32[4,128]{1,0:T(4,128)}, u32[]{:S(2)}) copy-start(s32[4,128]{1,0:T(4,128)} %param.7) | copy-start | bytes 6148
  39.7 16.3 %collective-permute-start.4 = (f32[128,1214]{0,1:T(8,128)}, f32[128,1214]{0,1:T(8,128)S(1)}, u32[]{:S(2)}, u32[]{:S(2)}) collective-permute-start(f32[128,1214]{0,1:T(8,128)} %copy.25), channel_id=1, source_target_pairs={{0,8},{8,0},{4,12},{12,4},{1,9},{9,1},{5,13},{13,5},{2,10},{10,2},... | collective-permute-start | bytes 1864712 | tf_op jit(solution)/shard_map/ppermute | solution.py:27
  57.6 2.4 %copy-start.1 = (f32[4,256,511]{2,1,0:T(8,128)S(1)}, f32[4,256,511]{2,1,0:T(8,128)}, u32[]{:S(2)}) copy-start(f32[4,256,511]{2,1,0:T(8,128)} %reshape.1315) | copy-start | bytes 6279172
  60.0 2.1 %copy-start.2 = (f32[4,256,511]{2,1,0:T(8,128)S(1)}, f32[4,256,511]{2,1,0:T(8,128)}, u32[]{:S(2)}) copy-start(f32[4,256,511]{2,1,0:T(8,128)} %reshape.1338) | copy-start | bytes 6279172

commit v2 on v1

--- a/solution.py
+++ b/solution.py
@@ -93,21 +93,18 @@
     return jnp.einsum("mk,mkl->ml", template_weight, onehot, precision=lax.Precision.HIGHEST)
 
 
-def toeplitz_band(pattern, block_len):
-    templ_count, period = pattern.shape
-    tiled = jnp.tile(pattern, (1, block_len))[:, : block_len * (period - 1)]
-    rows_view = tiled.reshape(templ_count, block_len, period - 1)[:, :, :block_len]
-    return jnp.swapaxes(rows_view, 1, 2)
-
-
 def make_bands(lag_weight):
     templ_count, tap_count = lag_weight.shape
     block_len = 2 * tap_count
-    spare = jnp.zeros((templ_count, block_len - tap_count), jnp.float32)
-    empty = jnp.zeros((templ_count, block_len), jnp.float32)
-    pattern_now = jnp.concatenate([lag_weight, spare, empty], axis=1)
-    pattern_next = jnp.concatenate([empty, lag_weight, spare], axis=1)
-    return (toeplitz_band(pattern_now, block_len), toeplitz_band(pattern_next, block_len))
+    position = jnp.arange(block_len, dtype=jnp.int32)
+    lag = position[:, None] - position[None, :]
+    padded = jnp.concatenate([lag_weight, jnp.zeros((templ_count, 1), jnp.float32)], axis=1)
+
+    def band(lag):
+        index = jnp.where((lag >= 0) & (lag < tap_count), lag, tap_count)
+        return padded[:, index]
+
+    return (band(lag), band(lag + block_len))
 
 
 def filter_blocks(padded_rows, lag_weight):

time: 66.3 us -> 526 us (7.93)
  local copies, waits for them, and re-layouts: 21.9 us -> 482 us
    gather x0 -> x4, local copies, waits for them, and re-layouts: none -> 472 us  [band(): return padded[:, index]]
    reshape x2 -> x0, local copies, waits for them, and re-layouts: 8.76 us -> none  [toeplitz_band(): tiled.reshape(templ_count, block_len, period - 1)[:, :, :block_len]]
  transfers between devices with their start and end apart: 5 -> 5, of which waited for: 4 -> 3; matrix products, arithmetic and copies ran while one was open for 24% -> 91% of each run, Pallas kernels for 0% -> 0%
where the time goes in v2:
time: 526 us; the launch traced here: 525 us
  local copies, waits for them, and re-layouts  482 us (92%)
  other arithmetic  18.6 us (4%)
  waiting for transfers between devices  10.7 us (2%)
  starting transfers between devices  8.69 us (2%)
    gather x4, local copies, waits for them, and re-layouts, band(): return padded[:, index]  472 us
  transfers between devices with their start and end apart: 5, of which 3 were waited for; matrix products, arithmetic and copies ran while one was open for 91% of the time, Pallas kernels for 0%

profile of v2, /device:TPU:0, one launch (start us, length us, event | category | flops | bytes accessed | tf_op | source)
XLA Modules:
  0.0 524.8 jit_solution(857124872549897749)
XLA Ops:
  0.0 1.2 fusion.101
  1.2 3.1 collective-permute-start
  4.3 1.0 fusion.55
  5.3 1.0 fusion.54
  6.3 2.7 collective-permute-start.1
  9.2 1.7 collective-permute-done.1
  10.9 1.2 subtract_multiply_fusion
  12.1 1.3 collective-permute-start.2
  13.4 7.2 %collective-permute-done.2 = f32[128,436]{1,0:T(8,128)S(1)} collective-permute-done((f32[128,436]{1,0:T(8,128)S(1)}, f32[128,436]{1,0:T(8,128)S(1)}, u32[]{:S(2)}, u32[]{:S(2)}) %collective-permute-start.2) | collective-permute-done | bytes 223264 | tf_op jit(solution)/shard_map/ppermute | solution.py:17
  20.6 0.5 reshape.1369
  21.1 0.6 slice_bitcast_fusion.12
  21.7 0.6 pad_maximum_fusion.1
  22.3 0.5 reshape.1370
  22.9 0.6 pad_maximum_fusion.2
  23.5 0.5 reshape.1371
  24.1 0.3 fusion.3
  24.3 0.5 reshape.1372
  24.9 0.3 pad_maximum_fusion.3
  25.5 0.3 pad_maximum_fusion.4
  26.1 0.3 slice_select_fusion.12
  26.4 0.3 fusion.2
  27.1 0.3 slice_select_fusion.10
  27.4 0.3 slice_select_fusion.9
  27.7 0.3 fusion.1
  28.2 0.3 slice_select_fusion.7
  28.5 0.3 slice_select_fusion.6
  28.8 0.3 slice_select_fusion.5
  29.1 0.3 fusion
  29.6 0.3 slice_select_fusion.3
  29.9 0.3 slice_select_fusion.2
  30.2 0.3 slice_select_fusion.1
  30.5 0.3 slice_select_fusion
  33.6 0.4 slice_select_fusion.16
  35.2 1.8 collective-permute-done.3
  38.3 0.3 fusion.6
  38.6 1.1 copy.36
  39.7 1.5 collective-permute-start.4
  41.3 0.3 fusion.19
  41.8 217.1 %gather_fusion = f32[65536,4]{1,0:T(8,128)} fusion(f32[4,129]{0,1:T(8,128)S(1)} %concatenate.51, s32[65536]{0:T(1024)S(1)} %broadcast_clamp_fusion.1), kind=kCustom, calls=%fused_computation | custom fusion | bytes 2359296 | tf_op jit(solution)/shard_map/gather | solution.py:105
  258.9 19.0 %copy.46 = f32[4,256,256,1]{1,2,3,0:T(8,128)S(1)} copy(f32[4,256,256,1]{0,2,1,3:T(8,128)} %bitcast.376) | data formatting | bytes 2097152 | tf_op jit(solution)/shard_map/gather | solution.py:105
  277.9 217.1 %gather_fusion.1 = f32[65536,4]{1,0:T(8,128)} fusion(f32[4,129]{0,1:T(8,128)S(1)} %concatenate.51, s32[65536]{0:T(1024)S(1)} %broadcast_clamp_fusion), kind=kCustom, calls=%fused_computation.1 | custom fusion | bytes 2359296 | tf_op jit(solution)/shard_map/gather | solution.py:105
  495.0 19.0 %copy.47 = f32[4,256,256,1]{1,2,3,0:T(8,128)S(1)} copy(f32[4,256,256,1]{0,2,1,3:T(8,128)} %bitcast.375) | data formatting | bytes 2097152 | tf_op jit(solution)/shard_map/gather | solution.py:105
  514.0 1.3 copy.37
  516.7 1.1 fusion.8
  517.7 1.3 copy.54
  519.1 1.8 fusion.9
  520.9 1.9 convolution_add_fusion
  522.8 2.0 copy.43
  (70 shorter events, 8.4 us)
Async XLA Ops:
  0.0 41.3 %copy-start = (f32[4,128]{1,0:T(4,128)S(1)}, f32[4,128]{1,0:T(4,128)}, u32[]{:S(2)}) copy-start(f32[4,128]{1,0:T(4,128)} %param.6) | copy-start | bytes 6148
  1.2 5.1 collective-permute-start
  6.3 4.5 collective-permute-start.1
  12.1 8.5 %collective-permute-start.2 = (f32[128,436]{1,0:T(8,128)S(1)}, f32[128,436]{1,0:T(8,128)S(1)}, u32[]{:S(2)}, u32[]{:S(2)}) collective-permute-start(f32[128,436]{1,0:T(8,128)S(1)} %slice.456), channel_id=1, source_target_pairs={{1,0},{2,1},{3,2},{5,4},{6,5},{7,6},{9,8},{10,9},{11,10},{13,12},{... | collective-permute-start | bytes 669704 | tf_op jit(solution)/shard_map/ppermute | solution.py:17
  34.8 2.2 collective-permute-start.3
  38.3 3.0 copy-start.2
  39.7 474.3 %collective-permute-start.4 = (f32[128,1214]{0,1:T(8,128)}, f32[128,1214]{0,1:T(8,128)}, u32[]{:S(2)}, u32[]{:S(2)}) collective-permute-start(f32[128,1214]{0,1:T(8,128)} %copy.36), channel_id=1, source_target_pairs={{0,8},{8,0},{4,12},{12,4},{1,9},{9,1},{5,13},{13,5},{2,10},{10,2},... | collective-permute-start | bytes 1864712 | tf_op jit(solution)/shard_map/ppermute | solution.py:27
  522.8 2.0 copy-start.1

commit v3 on v2

--- a/solution.py
+++ b/solution.py
@@ -93,18 +93,32 @@
     return jnp.einsum("mk,mkl->ml", template_weight, onehot, precision=lax.Precision.HIGHEST)
 
 
+def skewed(pattern, block_len):
+    templ_count, length = pattern.shape
+    current = jnp.broadcast_to(pattern[:, None, :], (templ_count, block_len, length))
+    offsets = block_len - 1 - jnp.arange(block_len, dtype=jnp.int32)
+    stride = 1
+    while stride < block_len:
+        chosen = (offsets // stride % 2 == 1)[None, :, None]
+        length = current.shape[2] - stride
+        current = jnp.where(chosen, current[:, :, stride:], current[:, :, :length])
+        stride = stride * 2
+    return current
+
+
 def make_bands(lag_weight):
     templ_count, tap_count = lag_weight.shape
     block_len = 2 * tap_count
-    position = jnp.arange(block_len, dtype=jnp.int32)
-    lag = position[:, None] - position[None, :]
-    padded = jnp.concatenate([lag_weight, jnp.zeros((templ_count, 1), jnp.float32)], axis=1)
-
-    def band(lag):
-        index = jnp.where((lag >= 0) & (lag < tap_count), lag, tap_count)
-        return padded[:, index]
-
-    return (band(lag), band(lag + block_len))
+    span = 2 * block_len - 1
+    lead = jnp.zeros((templ_count, block_len - 1), jnp.float32)
+    pattern_now = jnp.concatenate(
+        [lead, lag_weight, jnp.zeros((templ_count, span - block_len + 1 - tap_count), jnp.float32)],
+        axis=1,
+    )
+    pattern_next = jnp.concatenate(
+        [lag_weight[:, 1:], jnp.zeros((templ_count, span - tap_count + 1), jnp.float32)], axis=1
+    )
+    return (skewed(pattern_now, block_len), skewed(pattern_next, block_len))
 
 
 def filter_blocks(padded_rows, lag_weight):
@@ -112,9 +126,9 @@
     row_total, length = padded_rows.shape
     block_len = band_now.shape[1]
     blocks = padded_rows.reshape(row_total, length // block_len, block_len)
-    result = jnp.einsum("rni,mit->rmnt", blocks[:, :-1], band_now, precision=lax.Precision.HIGHEST)
+    result = jnp.einsum("rni,mti->rmnt", blocks[:, :-1], band_now, precision=lax.Precision.HIGHEST)
     result = result + jnp.einsum(
-        "rni,mit->rmnt", blocks[:, 1:], band_next, precision=lax.Precision.HIGHEST
+        "rni,mti->rmnt", blocks[:, 1:], band_next, precision=lax.Precision.HIGHEST
     )
     return result.reshape(row_total, band_now.shape[0], -1)
 

time: 526 us -> 90 us (0.17)
  local copies, waits for them, and re-layouts: 482 us -> 18.1 us
  other arithmetic: 18.6 us -> 42.6 us
    gather x4 -> x0, local copies, waits for them, and re-layouts: 472 us -> none  [band(): return padded[:, index]]
    select_n x0 -> x7, other arithmetic: none -> 20.2 us  [skewed(): current = jnp.where(chosen, current[:, :, stride:], current[:, :, :length])]
  transfers between devices with their start and end apart: 5 -> 5, of which waited for: 3 -> 3; matrix products, arithmetic and copies ran while one was open for 91% -> 26% of each run, Pallas kernels for 0% -> 0%
where the time goes in v3:
time: 90 us; the launch traced here: 89.3 us
  other arithmetic  42.6 us (47%)
  local copies, waits for them, and re-layouts  18.1 us (20%)
  waiting for transfers between devices  11.5 us (13%)
  starting transfers between devices  8.9 us (10%)
  matrix products  7.69 us (9%)
    select_n x7, other arithmetic, skewed(): current = jnp.where(chosen, current[:, :, stride:], current[:, :, :length])  20.2 us
    select_n x30, other arithmetic, shift_rows(): jnp.where(chosen[:, None], current[:, stride:], current[:, :length])  8.26 us
    ppermute x4, starting transfers between devices, swapped(): return lax.ppermute(block, axis, route)  7.43 us
    ppermute x1, waiting for transfers between devices, from_behind(): lax.ppermute(value, axis, [(source, source + steps) for source in range(l...  7.02 us
    add x7, other arithmetic, local_level(): return lower_rows + shift_rows(upper_rows, level_offsets, window)  4.84 us
    reshape x3, local copies, waits for them, and re-layouts, local_level(): groups = spectra.reshape(row_total // (2 * row_count), 2, row_count, length)  4.58 us
    ppermute x4, waiting for transfers between devices, swapped(): return lax.ppermute(block, axis, route)  4.44 us
    dot_general x1, matrix products, filter_blocks(): jnp.einsum('rni,mti->rmnt', blocks[:, :-1], band_now, precision=lax.Preci...  3.5 us
  transfers between devices with their start and end apart: 5, of which 3 were waited for; matrix products, arithmetic and copies ran while one was open for 26% of the time, Pallas kernels for 0%

profile of v3, /device:TPU:0, one launch (start us, length us, event | category | flops | bytes accessed | tf_op | source)
XLA Modules:
  0.0 89.3 jit_solution(12922844464098097299)
XLA Ops:
  0.0 1.2 %fusion.116 = (f32[128]{0:T(128)S(1)}, f32[128]{0:T(128)S(1)}) fusion(f32[128,1024]{1,0:T(8,128)} %param.4), kind=kLoop, calls=%fused_computation.475 | loop fusion | flops 392960 | bytes 525312 | tf_op jit(solution)/shard_map/reduce_sum | solution.py:141
  1.2 3.1 %collective-permute-start = (f32[2,128]{1,0:T(2,128)S(1)}, f32[2,128]{1,0:T(2,128)S(1)}, u32[]{:S(2)}, u32[]{:S(2)}) collective-permute-start(f32[2,128]{1,0:T(2,128)S(1)} %pad_maximum_fusion.11), channel_id=1, source_target_pairs={{0,1},{1,0},{2,3},{3,2},{4,5},{5,4},{6,7},{7,6},{8,9},{9,8},{10,11... | collective-permute-start | bytes 3080 | tf_op jit(solution)/shard_map/ppermute | solution.py:27
  4.4 1.0 %fusion.70 = (pred[128]{0:T(512)(128)(4,1)S(1)}, pred[128]{0:T(512)(128)(4,1)S(1)}, pred[128]{0:T(512)(128)(4,1)S(1)}, pred[128]{0:T(512)(128)(4,1)S(1)}, pred[1...) fusion(s32[9,128]{1,0:T(8,128)} %param.5), kind=kLoop, calls=%fused_computation.411 | loop fusion | flops 46720 | bytes 6400 | tf_op jit(solution)/shard_map/eq | solution.py:45
  5.4 1.0 %fusion.69 = (pred[128]{0:T(512)(128)(4,1)S(1)}, pred[128]{0:T(512)(128)(4,1)S(1)}, pred[128]{0:T(512)(128)(4,1)S(1)}, pred[128]{0:T(512)(128)(4,1)S(1)}, pred[1...) fusion(s32[9,128]{1,0:T(8,128)} %param.5), kind=kLoop, calls=%fused_computation.410 | loop fusion | flops 51328 | bytes 6016 | tf_op jit(solution)/shard_map/eq | solution.py:45
  6.3 1.0 %fusion.18 = f32[4,1,128]{2,1,0:T(1,128)S(1)} fusion(f32[4,128,1]{1,2,0:T(1,128)S(1)} %bitcast.365, s32[4,128]{1,0:T(4,128)} %param.7), kind=kOutput, calls=%fused_computation.110 | convolution fusion | flops 851968 | bytes 6144 | tf_op jit(solution)/shard_map/mk,mkl->ml/dot_general | solution.py:93
  7.7 0.6 broadcast_select_fusion
  8.3 1.2 %slice_select_fusion.4 = (f32[4,256,508]{2,1,0:T(8,128)S(1)}, f32[4,256,508]{2,1,0:T(8,128)S(1)}) fusion(f32[4,256,510]{2,1,0:T(8,128)S(1)} %get-tuple-element.80, pred[256]{0:T(512)(128)(4,1)S(1)} %fusion.34, f32[4,256,510]{2,1,0:T(8,128)S(1)} %get-tuple-element.81), kind=kLoop, calls=%fused_computation.4 | loop fusion | flops 1040384 | bytes 12484864 | tf_op jit(solution)/shard_map/jit(_where)/select_n | solution.py:104
  9.5 1.2 %slice_select_fusion.3 = (f32[4,256,504]{2,1,0:T(8,128)S(1)}, f32[4,256,504]{2,1,0:T(8,128)S(1)}) fusion(f32[4,256,508]{2,1,0:T(8,128)S(1)} %get-tuple-element.78, pred[256]{0:T(512)(128)(4,1)S(1)} %fusion.33, f32[4,256,508]{2,1,0:T(8,128)S(1)} %get-tuple-element.79), kind=kLoop, calls=%fused_computation.3 | loop fusion | flops 1032192 | bytes 12386560 | tf_op jit(solution)/shard_map/jit(_where)/select_n | solution.py:104
  10.7 2.5 %slice_select_fusion.2 = (f32[4,256,496]{2,1,0:T(8,128)S(1)}, f32[4,256,496]{2,1,0:T(8,128)}) fusion(f32[4,256,504]{2,1,0:T(8,128)S(1)} %get-tuple-element.76, pred[256]{0:T(512)(128)(4,1)S(1)} %fusion.32, f32[4,256,504]{2,1,0:T(8,128)S(1)} %get-tuple-element.77), kind=kLoop, calls=%fused_computation.2 | loop fusion | flops 1015808 | bytes 12189952 | tf_op jit(solution)/shard_map/jit(_where)/select_n | solution.py:104
  13.2 2.7 %collective-permute-start.1 = (f32[2,128]{1,0:T(2,128)S(1)}, f32[2,128]{1,0:T(2,128)S(1)}, u32[]{:S(2)}, u32[]{:S(2)}) collective-permute-start(f32[2,128]{1,0:T(2,128)S(1)} %fusion.115), channel_id=1, source_target_pairs={{0,2},{2,0},{1,3},{3,1},{4,6},{6,4},{5,7},{7,5},{8,10},{10,8},{9,1... | collective-permute-start | bytes 3080 | tf_op jit(solution)/shard_map/ppermute | solution.py:27
  15.9 1.9 %collective-permute-done.1 = f32[2,128]{1,0:T(2,128)S(1)} collective-permute-done((f32[2,128]{1,0:T(2,128)S(1)}, f32[2,128]{1,0:T(2,128)S(1)}, u32[]{:S(2)}, u32[]{:S(2)}) %collective-permute-start.1) | collective-permute-done | bytes 1056 | tf_op jit(solution)/shard_map/ppermute | solution.py:27
  17.9 1.5 %collective-permute-start.2 = (f32[128,436]{1,0:T(8,128)S(1)}, f32[128,436]{1,0:T(8,128)S(1)}, u32[]{:S(2)}, u32[]{:S(2)}) collective-permute-start(f32[128,436]{1,0:T(8,128)S(1)} %slice.604), channel_id=1, source_target_pairs={{1,0},{2,1},{3,2},{5,4},{6,5},{7,6},{9,8},{10,9},{11,10},{13,12},{... | collective-permute-start | bytes 669704 | tf_op jit(solution)/shard_map/ppermute | solution.py:17
  19.4 7.0 %collective-permute-done.2 = f32[128,436]{1,0:T(8,128)S(1)} collective-permute-done((f32[128,436]{1,0:T(8,128)S(1)}, f32[128,436]{1,0:T(8,128)S(1)}, u32[]{:S(2)}, u32[]{:S(2)}) %collective-permute-start.2) | collective-permute-done | bytes 223264 | tf_op jit(solution)/shard_map/ppermute | solution.py:17
  26.5 0.9 %pad_maximum_fusion = f32[128,1460]{1,0:T(8,128)} fusion(f32[128,436]{1,0:T(8,128)S(1)} %collective-permute-done.2, f32[128,1024]{1,0:T(8,128)S(1)} %subtract_multiply_fusion), kind=kLoop, calls=%fused_computation.40 | loop fusion | flops 186880 | bytes 1495040 | tf_op jit(solution)/shard_map/concatenate | solution.py:155
  27.4 1.6 %reshape.1492 = f32[64,2,1,1460]{3,1,0,2:T(2,128)S(1)} reshape(f32[128,1460]{1,0:T(8,128)} %pad_maximum_fusion) | data formatting | bytes 1495040 | tf_op jit(solution)/shard_map/reshape | solution.py:54
  29.0 0.6 slice_bitcast_fusion.12
  29.6 0.6 pad_maximum_fusion.1
  30.2 1.4 %reshape.1493 = f32[128,1459]{1,0:T(8,128)} reshape(f32[64,2,1459]{2,1,0:T(2,128)S(1)} %pad_maximum_fusion.1) | data formatting | bytes 1494016 | tf_op jit(solution)/shard_map/reshape | solution.py:58
  31.7 1.5 %pad_maximum_fusion.2 = f32[64,2,1460]{2,1,0:T(2,128)} fusion(f32[64,1,1460]{2,1,0:T(1,128)S(1)} %get-tuple-element.19), kind=kLoop, calls=%fused_computation.42 | loop fusion | flops 186880 | bytes 1121280 | tf_op jit(solution)/shard_map/concatenate | solution.py:59
  33.2 1.7 %reshape.1494 = f32[128,1460]{1,0:T(8,128)S(1)} reshape(f32[64,2,1460]{2,1,0:T(2,128)} %pad_maximum_fusion.2) | data formatting | bytes 1495040 | tf_op jit(solution)/shard_map/reshape | solution.py:59
  34.9 2.3 %fusion.10 = f32[128,1459]{1,0:T(8,128)} fusion(f32[128,1459]{1,0:T(8,128)} %reshape.1493, f32[128,1460]{1,0:T(8,128)S(1)} %reshape.1494, pred[128]{0:T(512)(128)(4,1)S(1)} %get-tuple-element.61), kind=kLoop, calls=%fused_computation.39 | loop fusion | flops 373504 | bytes 2988160 | tf_op jit(solution)/shard_map/add | solution.py:60
  37.2 1.6 %reshape.1495 = f32[32,2,2,1459]{3,2,1,0:T(2,128)S(1)} reshape(f32[128,1459]{1,0:T(8,128)} %fusion.10) | data formatting | bytes 1494016 | tf_op jit(solution)/shard_map/reshape | solution.py:54
  38.8 0.3 pad_maximum_fusion.3
  39.1 1.2 %reshape.1496 = f32[128,1456]{1,0:T(8,128)} reshape(f32[32,4,1456]{2,1,0:T(4,128)S(1)} %pad_maximum_fusion.3) | data formatting | bytes 1490944 | tf_op jit(solution)/shard_map/reshape | solution.py:58
  40.3 1.2 %pad_maximum_fusion.4 = f32[32,4,1459]{2,1,0:T(4,128)} fusion(f32[32,2,1459]{2,1,0:T(2,128)S(1)} %get-tuple-element.17), kind=kLoop, calls=%fused_computation.44 | loop fusion | flops 186752 | bytes 1120512 | tf_op jit(solution)/shard_map/concatenate | solution.py:59
  41.5 1.4 %reshape.1497 = f32[128,1459]{1,0:T(8,128)S(1)} reshape(f32[32,4,1459]{2,1,0:T(4,128)} %pad_maximum_fusion.4) | data formatting | bytes 1494016 | tf_op jit(solution)/shard_map/reshape | solution.py:59
  42.9 0.3 slice_select_fusion.26
  43.2 0.8 copy-done.5
  44.1 1.2 %fusion.9 = f32[128,1456]{1,0:T(8,128)} fusion(f32[128,1456]{1,0:T(8,128)S(1)} %copy-done.5, f32[128,1458]{1,0:T(8,128)S(1)} %slice_select_fusion.26, pred[128]{0:T(512)(128)(4,1)S(1)} %get-tuple-element.54), kind=kLoop, calls=%fused_computation.36 | loop fusion | flops 372736 | bytes 2982016 | tf_op jit(solution)/shard_map/add | solution.py:60
  45.2 1.4 %reshape.1498 = f32[16,2,4,1456]{3,2,1,0:T(4,128)S(1)} reshape(f32[128,1456]{1,0:T(8,128)} %fusion.9) | data formatting | bytes 1490944 | tf_op jit(solution)/shard_map/reshape | solution.py:54
  47.4 0.3 fusion.8
  47.9 0.3 slice_select_fusion.21
  48.2 0.3 slice_select_fusion.20
  48.8 0.3 fusion.7
  49.3 0.3 slice_select_fusion.17
  49.6 0.3 slice_select_fusion.16
  53.0 0.5 slice_select_fusion.31
  54.7 0.9 %copy-done.2 = f32[4,256,496]{2,1,0:T(8,128)S(1)} copy-done((f32[4,256,496]{2,1,0:T(8,128)S(1)}, f32[4,256,496]{2,1,0:T(8,128)}, u32[]{:S(2)}) %copy-start.2) | copy-done | bytes 2031640
  55.6 3.2 %slice_select_fusion.1 = (f32[4,256,480]{2,1,0:T(8,128)}, f32[4,256,480]{2,1,0:T(8,128)}) fusion(f32[4,256,496]{2,1,0:T(8,128)S(1)} %get-tuple-element.74, pred[256]{0:T(512)(128)(4,1)S(1)} %fusion.31, f32[4,256,496]{2,1,0:T(8,128)S(1)} %copy-done.2), kind=kLoop, calls=%fused_computation.1 | loop fusion | flops 983040 | bytes 11796736 | tf_op jit(solution)/shard_map/jit(_where)/select_n | solution.py:104
  60.1 0.3 fusion.13
  60.7 1.6 %collective-permute-start.4 = (f32[128,1214]{0,1:T(8,128)S(1)}, f32[128,1214]{0,1:T(8,128)}, u32[]{:S(2)}, u32[]{:S(2)}) collective-permute-start(f32[128,1214]{0,1:T(8,128)S(1)} %copy.25), channel_id=1, source_target_pairs={{0,8},{8,0},{4,12},{12,4},{1,9},{9,1},{5,13},{13,5},{2,10},{10,2},... | collective-permute-start | bytes 1864712 | tf_op jit(solution)/shard_map/ppermute | solution.py:27
  62.3 5.6 %slice_select_fusion = (f32[4,256,448]{2,1,0:T(8,128)}, f32[4,256,448]{2,1,0:T(8,128)}) fusion(f32[4,256,480]{2,1,0:T(8,128)S(1)} %copy-done.3, pred[256]{0:T(512)(128)(4,1)S(1)} %fusion.30, f32[4,256,480]{2,1,0:T(8,128)} %get-tuple-element.73), kind=kLoop, calls=%fused_computation | loop fusion | flops 917504 | bytes 11010304 | tf_op jit(solution)/shard_map/jit(_where)/select_n | solution.py:104
  67.9 5.9 %slice_select_fusion.10 = (f32[4,256,384]{2,1,0:T(8,128)}, f32[4,256,384]{2,1,0:T(8,128)}) fusion(f32[4,256,448]{2,1,0:T(8,128)} %get-tuple-element.70, pred[256]{0:T(512)(128)(4,1)S(1)} %fusion.29, f32[4,256,448]{2,1,0:T(8,128)} %get-tuple-element.71), kind=kLoop, calls=%fused_computation.11 | loop fusion | flops 786432 | bytes 9437440 | tf_op jit(solution)/shard_map/jit(_where)/select_n | solution.py:104
  73.8 2.6 %collective-permute-done.4 = f32[128,1214]{0,1:T(8,128)} collective-permute-done((f32[128,1214]{0,1:T(8,128)S(1)}, f32[128,1214]{0,1:T(8,128)}, u32[]{:S(2)}, u32[]{:S(2)}) %collective-permute-start.4) | collective-permute-done | bytes 621600 | tf_op jit(solution)/shard_map/ppermute | solution.py:27
  76.4 1.3 %copy.26 = f32[128,1214]{1,0:T(8,128)S(1)} copy(f32[128,1214]{0,1:T(8,128)} %collective-permute-done.4) | data formatting | bytes 1243136 | tf_op jit(solution)/shard_map/ppermute | solution.py:27
  79.6 3.5 %fusion.4 = f32[4,256,128,4]{2,1,3,0:T(8,128)S(1)} fusion(f32[4,256,384]{2,1,0:T(8,128)} %get-tuple-element.69, f32[128,5,256]{0,2,1:T(8,128)S(1)} %bitcast.370, pred[256]{0:T(512)(128)(4,1)S(1)} %fusion.28), kind=kOutput, calls=%fused_computation.18 | convolution fusion | flops 1610874880 | bytes 4719104 | tf_op jit(solution)/shard_map/rni,mti->rmnt/dot_general | solution.py:129
  83.1 3.2 %convolution_add_fusion = f32[4,256,128,4]{2,1,3,0:T(8,128)} fusion(f32[4,256,128,4]{2,1,3,0:T(8,128)S(1)} %fusion.4, f32[4,256,384]{2,1,0:T(8,128)S(1)} %copy-done.4, f32[128,5,256]{0,2,1:T(8,128)S(1)} %bitcast.371, pred[256]{0:T(512)(128)(4,1)S(1)} %fusion.28), kind=kOutput, calls=%fused_computation.10 | convolution fusion | flops 1611399168 | bytes 6816256 | tf_op jit(solution)/shard_map/rni,mti->rmnt/dot_general | solution.py:130
  86.3 3.0 %copy.31 = f32[128,4,1024]{2,1,0:T(4,128)} copy(f32[128,4,1024]{0,2,1:T(8,128)} %bitcast.366) | data formatting | bytes 4194304 | tf_op jit(solution)/shard_map/reshape | solution.py:133
  (88 shorter events, 9.7 us)
Async XLA Ops:
  0.0 6.3 %copy-start = (f32[4,128]{1,0:T(4,128)S(1)}, f32[4,128]{1,0:T(4,128)}, u32[]{:S(2)}) copy-start(f32[4,128]{1,0:T(4,128)} %param.6) | copy-start | bytes 6148
  1.2 12.0 %collective-permute-start = (f32[2,128]{1,0:T(2,128)S(1)}, f32[2,128]{1,0:T(2,128)S(1)}, u32[]{:S(2)}, u32[]{:S(2)}) collective-permute-start(f32[2,128]{1,0:T(2,128)S(1)} %pad_maximum_fusion.11), channel_id=1, source_target_pairs={{0,1},{1,0},{2,3},{3,2},{4,5},{5,4},{6,7},{7,6},{8,9},{9,8},{10,11... | collective-permute-start | bytes 3080 | tf_op jit(solution)/shard_map/ppermute | solution.py:27
  10.7 7.1 %copy-start.6 = (f32[128,1024]{1,0:T(8,128)S(1)}, f32[128,1024]{1,0:T(8,128)}, u32[]{:S(2)}) copy-start(f32[128,1024]{1,0:T(8,128)} %param.4) | copy-start | bytes 1572868
  13.2 4.5 %collective-permute-start.1 = (f32[2,128]{1,0:T(2,128)S(1)}, f32[2,128]{1,0:T(2,128)S(1)}, u32[]{:S(2)}, u32[]{:S(2)}) collective-permute-start(f32[2,128]{1,0:T(2,128)S(1)} %fusion.115), channel_id=1, source_target_pairs={{0,2},{2,0},{1,3},{3,1},{4,6},{6,4},{5,7},{7,5},{8,10},{10,8},{9,1... | collective-permute-start | bytes 3080 | tf_op jit(solution)/shard_map/ppermute | solution.py:27
  17.9 8.5 %collective-permute-start.2 = (f32[128,436]{1,0:T(8,128)S(1)}, f32[128,436]{1,0:T(8,128)S(1)}, u32[]{:S(2)}, u32[]{:S(2)}) collective-permute-start(f32[128,436]{1,0:T(8,128)S(1)} %slice.604), channel_id=1, source_target_pairs={{1,0},{2,1},{3,2},{5,4},{6,5},{7,6},{9,8},{10,9},{11,10},{13,12},{... | collective-permute-start | bytes 669704 | tf_op jit(solution)/shard_map/ppermute | solution.py:17
  42.9 1.1 %copy-start.5 = (f32[128,1456]{1,0:T(8,128)S(1)}, f32[128,1456]{1,0:T(8,128)}, u32[]{:S(2)}) copy-start(f32[128,1456]{1,0:T(8,128)} %reshape.1496) | copy-start | bytes 2236420
  54.0 1.6 %copy-start.2 = (f32[4,256,496]{2,1,0:T(8,128)S(1)}, f32[4,256,496]{2,1,0:T(8,128)}, u32[]{:S(2)}) copy-start(f32[4,256,496]{2,1,0:T(8,128)} %get-tuple-element.75) | copy-start | bytes 6094852
  54.5 4.3 %collective-permute-start.3 = (f32[128,1277]{1,0:T(8,128)S(1)}, f32[128,1277]{1,0:T(8,128)S(1)}, u32[]{:S(2)}, u32[]{:S(2)}) collective-permute-start(f32[128,1277]{1,0:T(8,128)S(1)} %fusion.14), channel_id=1, source_target_pairs={{0,4},{4,0},{8,12},{12,8},{1,5},{5,1},{9,13},{13,9},{2,6},{6,2},{1... | collective-permute-start | bytes 1961480 | tf_op jit(solution)/shard_map/ppermute | solution.py:27
  60.1 2.1 %copy-start.3 = (f32[4,256,480]{2,1,0:T(8,128)S(1)}, f32[4,256,480]{2,1,0:T(8,128)}, u32[]{:S(2)}) copy-start(f32[4,256,480]{2,1,0:T(8,128)} %get-tuple-element.72) | copy-start | bytes 5898244
  60.7 15.7 %collective-permute-start.4 = (f32[128,1214]{0,1:T(8,128)S(1)}, f32[128,1214]{0,1:T(8,128)}, u32[]{:S(2)}, u32[]{:S(2)}) collective-permute-start(f32[128,1214]{0,1:T(8,128)S(1)} %copy.25), channel_id=1, source_target_pairs={{0,8},{8,0},{4,12},{12,4},{1,9},{9,1},{5,13},{13,5},{2,10},{10,2},... | collective-permute-start | bytes 1864712 | tf_op jit(solution)/shard_map/ppermute | solution.py:27
  79.6 3.5 %copy-start.4 = (f32[4,256,384]{2,1,0:T(8,128)S(1)}, f32[4,256,384]{2,1,0:T(8,128)}, u32[]{:S(2)}) copy-start(f32[4,256,384]{2,1,0:T(8,128)} %get-tuple-element.68) | copy-start | bytes 4718596
  86.3 3.1 %copy-start.1 = (f32[4,128]{1,0:T(4,128)S(1)}, f32[4,128]{1,0:T(4,128)}, u32[]{:S(2)}) copy-start(f32[4,128]{1,0:T(4,128)} %param.6) | copy-start | bytes 6148

commit v4 on v1

--- a/solution.py
+++ b/solution.py
@@ -115,10 +115,9 @@
     row_total, length = padded_rows.shape
     block_len = band_now.shape[1]
     blocks = padded_rows.reshape(row_total, length // block_len, block_len)
-    result = jnp.einsum("rni,mit->rmnt", blocks[:, :-1], band_now, precision=lax.Precision.HIGHEST)
-    result = result + jnp.einsum(
-        "rni,mit->rmnt", blocks[:, 1:], band_next, precision=lax.Precision.HIGHEST
-    )
+    windows = jnp.concatenate([blocks[:, :-1], blocks[:, 1:]], axis=2)
+    band = jnp.concatenate([band_now, band_next], axis=1)
+    result = jnp.einsum("rni,mit->rmnt", windows, band, precision=lax.Precision.HIGHEST)
     return result.reshape(row_total, band_now.shape[0], -1)
 
 

time: 66.3 us -> 73.1 us (1.10)
  local copies, waits for them, and re-layouts: 21.9 us -> 29.7 us
  waiting for transfers between devices: 12 us -> 10.7 us
  matrix products: 4.26 us -> 5.29 us
  other arithmetic: 18.4 us -> 17.6 us
    unnamed x12 -> x16, local copies, waits for them, and re-layouts: 4.39 us -> 8.65 us
    transpose x0 -> x2, local copies, waits for them, and re-layouts: none -> 3.5 us  [toeplitz_band(): return jnp.swapaxes(rows_view, 1, 2)]
    ppermute x4, waiting for transfers between devices: 4.84 us -> 3.51 us  [swapped(): return lax.ppermute(block, axis, route)]
    dot_general x2 -> x1, matrix products: 3.96 us -> 4.99 us  [filter_blocks(): jnp.einsum('rni,mit->rmnt', windows, band, precision=lax.Precision.HIGHEST)]
    add x2, other arithmetic: 1.35 us -> 0.54 us  [cross_level(): return lower_rows + shift_rows(upper_rows, level_offsets, window)]
  transfers between devices with their start and end apart: 5 -> 5, of which waited for: 4 -> 3; matrix products, arithmetic and copies ran while one was open for 24% -> 31% of each run, Pallas kernels for 0% -> 0%
where the time goes in v4:
time: 73.1 us; the launch traced here: 72.7 us
  local copies, waits for them, and re-layouts  29.7 us (41%)
  other arithmetic  17.6 us (24%)
  waiting for transfers between devices  10.7 us (15%)
  starting transfers between devices  8.71 us (12%)
  matrix products  5.29 us (7%)
    reshape x2, local copies, waits for them, and re-layouts, toeplitz_band(): tiled.reshape(templ_count, block_len, period - 1)[:, :, :block_len]  8.76 us
    unnamed x16, local copies, waits for them, and re-layouts  8.65 us
    select_n x30, other arithmetic, shift_rows(): jnp.where(chosen[:, None], current[:, stride:], current[:, :length])  8.24 us
    ppermute x4, starting transfers between devices, swapped(): return lax.ppermute(block, axis, route)  7.42 us
    ppermute x1, waiting for transfers between devices, from_behind(): lax.ppermute(value, axis, [(source, source + steps) for source in range(l...  7.2 us
    dot_general x1, matrix products, filter_blocks(): jnp.einsum('rni,mit->rmnt', windows, band, precision=lax.Precision.HIGHEST)  4.99 us
    ppermute x4, waiting for transfers between devices, swapped(): return lax.ppermute(block, axis, route)  3.51 us
    transpose x2, local copies, waits for them, and re-layouts, toeplitz_band(): return jnp.swapaxes(rows_view, 1, 2)  3.5 us
  transfers between devices with their start and end apart: 5, of which 3 were waited for; matrix products, arithmetic and copies ran while one was open for 31% of the time, Pallas kernels for 0%

profile of v4, /device:TPU:0, one launch (start us, length us, event | category | flops | bytes accessed | tf_op | source)
XLA Modules:
  0.0 72.7 jit_solution(1716343456372180652)
XLA Ops:
  0.0 1.2 %fusion.97 = (f32[128]{0:T(128)S(1)}, f32[128]{0:T(128)S(1)}) fusion(f32[128,1024]{1,0:T(8,128)} %param.4), kind=kLoop, calls=%fused_computation.397 | loop fusion | flops 392960 | bytes 525312 | tf_op jit(solution)/shard_map/reduce_sum | solution.py:129
  1.2 3.1 %collective-permute-start = (f32[2,128]{1,0:T(2,128)S(1)}, f32[2,128]{1,0:T(2,128)S(1)}, u32[]{:S(2)}, u32[]{:S(2)}) collective-permute-start(f32[2,128]{1,0:T(2,128)S(1)} %pad_maximum_fusion.13), channel_id=1, source_target_pairs={{0,1},{1,0},{2,3},{3,2},{4,5},{5,4},{6,7},{7,6},{8,9},{9,8},{10,11... | collective-permute-start | bytes 3080 | tf_op jit(solution)/shard_map/ppermute | solution.py:27
  4.3 0.9 %fusion.49 = (pred[128]{0:T(512)(128)(4,1)S(1)}, pred[128]{0:T(512)(128)(4,1)S(1)}, pred[128]{0:T(512)(128)(4,1)S(1)}, pred[128]{0:T(512)(128)(4,1)S(1)}, pred[1...) fusion(s32[9,128]{1,0:T(8,128)} %param.5), kind=kLoop, calls=%fused_computation.332 | loop fusion | flops 51328 | bytes 6016 | tf_op jit(solution)/shard_map/eq | solution.py:45
  5.3 1.0 %fusion.50 = (pred[128]{0:T(512)(128)(4,1)S(1)}, pred[128]{0:T(512)(128)(4,1)S(1)}, pred[128]{0:T(512)(128)(4,1)S(1)}, pred[128]{0:T(512)(128)(4,1)S(1)}, pred[1...) fusion(s32[9,128]{1,0:T(8,128)} %param.5), kind=kLoop, calls=%fused_computation.333 | loop fusion | flops 46720 | bytes 6400 | tf_op jit(solution)/shard_map/eq | solution.py:45
  6.3 2.7 %collective-permute-start.1 = (f32[2,128]{1,0:T(2,128)S(1)}, f32[2,128]{1,0:T(2,128)S(1)}, u32[]{:S(2)}, u32[]{:S(2)}) collective-permute-start(f32[2,128]{1,0:T(2,128)S(1)} %fusion.96), channel_id=1, source_target_pairs={{0,2},{2,0},{1,3},{3,1},{4,6},{6,4},{5,7},{7,5},{8,10},{10,8},{9,1... | collective-permute-start | bytes 3080 | tf_op jit(solution)/shard_map/ppermute | solution.py:27
  9.0 1.8 %collective-permute-done.1 = f32[2,128]{1,0:T(2,128)S(1)} collective-permute-done((f32[2,128]{1,0:T(2,128)S(1)}, f32[2,128]{1,0:T(2,128)S(1)}, u32[]{:S(2)}, u32[]{:S(2)}) %collective-permute-start.1) | collective-permute-done | bytes 1056 | tf_op jit(solution)/shard_map/ppermute | solution.py:27
  10.9 1.2 %subtract_multiply_fusion = f32[128,1024]{1,0:T(8,128)S(1)} fusion(f32[128,1024]{1,0:T(8,128)} %param.4, f32[128]{0:T(128)S(1)} %fusion.94, f32[128]{0:T(128)S(1)} %multiply_bitcast_fusion), kind=kLoop, calls=%fused_computation.76 | loop fusion | flops 262144 | bytes 1049600 | tf_op jit(solution)/shard_map/mul | solution.py:136
  12.1 1.3 %collective-permute-start.2 = (f32[128,436]{1,0:T(8,128)S(1)}, f32[128,436]{1,0:T(8,128)S(1)}, u32[]{:S(2)}, u32[]{:S(2)}) collective-permute-start(f32[128,436]{1,0:T(8,128)S(1)} %slice.472), channel_id=1, source_target_pairs={{1,0},{2,1},{3,2},{5,4},{6,5},{7,6},{9,8},{10,9},{11,10},{13,12},{... | collective-permute-start | bytes 669704 | tf_op jit(solution)/shard_map/ppermute | solution.py:17
  13.4 7.2 %collective-permute-done.2 = f32[128,436]{1,0:T(8,128)S(1)} collective-permute-done((f32[128,436]{1,0:T(8,128)S(1)}, f32[128,436]{1,0:T(8,128)S(1)}, u32[]{:S(2)}, u32[]{:S(2)}) %collective-permute-start.2) | collective-permute-done | bytes 223264 | tf_op jit(solution)/shard_map/ppermute | solution.py:17
  20.6 0.5 reshape.1317
  21.1 0.6 slice_bitcast_fusion.10
  21.7 0.6 pad_maximum_fusion.1
  22.3 0.5 reshape.1318
  22.9 0.6 pad_maximum_fusion.2
  23.5 0.5 reshape.1319
  24.0 0.3 fusion.8
  24.3 0.5 reshape.1320
  24.9 0.3 pad_maximum_fusion.3
  25.5 0.3 pad_maximum_fusion.4
  26.1 0.3 slice_select_fusion.12
  26.3 0.3 fusion.7
  27.4 0.3 slice_select_fusion.9
  27.7 0.3 fusion.6
  28.2 0.3 slice_select_fusion.7
  28.5 0.3 slice_select_fusion.6
  28.8 0.3 slice_select_fusion.5
  29.1 0.3 fusion.5
  29.6 0.3 slice_select_fusion.3
  29.9 0.3 slice_select_fusion.2
  30.5 0.3 slice_select_fusion
  33.5 0.4 slice_select_fusion.16
  34.9 0.3 fusion.14
  35.3 1.7 %collective-permute-done.3 = f32[128,1277]{1,0:T(8,128)S(1)} collective-permute-done((f32[128,1277]{1,0:T(8,128)S(1)}, f32[128,1277]{1,0:T(8,128)S(1)}, u32[]{:S(2)}, u32[]{:S(2)}) %collective-permute-start.3) | collective-permute-done | bytes 653856 | tf_op jit(solution)/shard_map/ppermute | solution.py:27
  38.6 1.1 %copy.25 = f32[128,1214]{0,1:T(8,128)} copy(f32[128,1214]{1,0:T(8,128)S(1)} %fusion.11) | data formatting | bytes 1243136 | tf_op jit(solution)/shard_map/add | solution.py:69
  39.7 1.5 %collective-permute-start.4 = (f32[128,1214]{0,1:T(8,128)}, f32[128,1214]{0,1:T(8,128)S(1)}, u32[]{:S(2)}, u32[]{:S(2)}) collective-permute-start(f32[128,1214]{0,1:T(8,128)} %copy.25), channel_id=1, source_target_pairs={{0,8},{8,0},{4,12},{12,4},{1,9},{9,1},{5,13},{13,5},{2,10},{10,2},... | collective-permute-start | bytes 1864712 | tf_op jit(solution)/shard_map/ppermute | solution.py:27
  41.2 1.9 %broadcast_bitcast_fusion = (f32[1,4,256,512]{3,2,1,0:T(8,128)}, f32[1,4,256,512]{3,2,1,0:T(8,128)S(1)}) fusion(f32[4,512]{1,0:T(4,128)S(1)} %get-tuple-element.67, f32[4,512]{1,0:T(4,128)S(1)} %get-tuple-element.66), kind=kLoop, calls=%fused_computation.9 | loop fusion | bytes 4210688
  43.0 2.9 %copy.41 = f32[1,4,256,512]{3,1,2,0:T(4,128)S(1)} copy(f32[1,4,256,512]{3,2,1,0:T(8,128)} %get-tuple-element.68) | data formatting | bytes 4194304
  46.0 1.5 %slice.470 = f32[4,130816]{1,0:T(4,128)} slice(f32[4,131072]{1,0:T(4,128)S(1)} %bitcast.367), slice={[0:4], [0:130816]} | slice | bytes 4186112 | tf_op jit(solution)/shard_map/slice | solution.py:98
  47.5 5.1 %reshape.1316 = f32[4,256,511]{2,1,0:T(8,128)} reshape(f32[4,130816]{1,0:T(4,128)} %slice.470) | data formatting | bytes 4186112 | tf_op jit(solution)/shard_map/reshape | solution.py:99
  52.6 1.4 %copy.40 = f32[1,4,256,512]{3,1,2,0:T(4,128)S(1)} copy(f32[1,4,256,512]{3,2,1,0:T(8,128)S(1)} %get-tuple-element.69) | data formatting | bytes 4194304
  54.1 3.7 %reshape.1315 = f32[4,256,511]{2,1,0:T(8,128)} reshape(f32[4,130816]{1,0:T(4,128)S(1)} %slice.468) | data formatting | bytes 4186112 | tf_op jit(solution)/shard_map/reshape | solution.py:99
  57.7 2.4 %slice_bitcast_fusion = f32[4,256,256]{1,2,0:T(8,128)} fusion(f32[4,256,511]{2,1,0:T(8,128)} %reshape.1316), kind=kLoop, calls=%fused_computation.4 | loop fusion | bytes 2097152 | tf_op jit(solution)/shard_map/transpose | solution.py:100
  60.2 1.1 %slice_bitcast_fusion.1 = f32[4,256,256]{1,2,0:T(8,128)} fusion(f32[4,256,511]{2,1,0:T(8,128)S(1)} %copy-done.2), kind=kLoop, calls=%fused_computation.5 | loop fusion | bytes 2097152 | tf_op jit(solution)/shard_map/transpose | solution.py:100
  63.1 0.4 copy.39
  63.7 1.0 %copy.38 = f32[128,4,256]{2,0,1:T(8,128)} copy(f32[128,4,256]{0,2,1:T(8,128)S(1)} %get-tuple-element.26) | data formatting | bytes 1048576
  64.7 1.0 %copy.37 = f32[128,4,256]{2,0,1:T(8,128)} copy(f32[128,4,256]{0,2,1:T(8,128)S(1)} %get-tuple-element.25) | data formatting | bytes 1048576
  65.7 5.0 %fusion = f32[4,256,128,4]{2,1,3,0:T(8,128)S(1)} fusion(f32[4,256,256]{1,2,0:T(8,128)S(1)} %copy-done.3, f32[4,256,256]{1,2,0:T(8,128)} %slice_bitcast_fusion.1, f32[128,4,256]{2,0,1:T(8,128)} %copy.38, f32[128,4,256]{2,0,1:T(8,128)} %copy.37), kind=kOutput, calls=%fused_computation.1 | convolution fusion | flops 3222011904 | bytes 5242880 | tf_op jit(solution)/shard_map/rni,mit->rmnt/dot_general | solution.py:120
  70.7 2.0 %copy.31 = f32[128,4,1024]{2,1,0:T(4,128)} copy(f32[128,4,1024]{0,2,1:T(8,128)S(1)} %bitcast.366) | data formatting | bytes 4194304 | tf_op jit(solution)/shard_map/reshape | solution.py:121
  (76 shorter events, 9.4 us)
Async XLA Ops:
  0.0 34.9 %copy-start = (f32[4,128]{1,0:T(4,128)S(1)}, f32[4,128]{1,0:T(4,128)}, u32[]{:S(2)}) copy-start(f32[4,128]{1,0:T(4,128)} %param.6) | copy-start | bytes 6148
  1.2 5.0 %collective-permute-start = (f32[2,128]{1,0:T(2,128)S(1)}, f32[2,128]{1,0:T(2,128)S(1)}, u32[]{:S(2)}, u32[]{:S(2)}) collective-permute-start(f32[2,128]{1,0:T(2,128)S(1)} %pad_maximum_fusion.13), channel_id=1, source_target_pairs={{0,1},{1,0},{2,3},{3,2},{4,5},{5,4},{6,7},{7,6},{8,9},{9,8},{10,11... | collective-permute-start | bytes 3080 | tf_op jit(solution)/shard_map/ppermute | solution.py:27
  6.3 4.5 %collective-permute-start.1 = (f32[2,128]{1,0:T(2,128)S(1)}, f32[2,128]{1,0:T(2,128)S(1)}, u32[]{:S(2)}, u32[]{:S(2)}) collective-permute-start(f32[2,128]{1,0:T(2,128)S(1)} %fusion.96), channel_id=1, source_target_pairs={{0,2},{2,0},{1,3},{3,1},{4,6},{6,4},{5,7},{7,5},{8,10},{10,8},{9,1... | collective-permute-start | bytes 3080 | tf_op jit(solution)/shard_map/ppermute | solution.py:27
  12.1 8.5 %collective-permute-start.2 = (f32[128,436]{1,0:T(8,128)S(1)}, f32[128,436]{1,0:T(8,128)S(1)}, u32[]{:S(2)}, u32[]{:S(2)}) collective-permute-start(f32[128,436]{1,0:T(8,128)S(1)} %slice.472), channel_id=1, source_target_pairs={{1,0},{2,1},{3,2},{5,4},{6,5},{7,6},{9,8},{10,9},{11,10},{13,12},{... | collective-permute-start | bytes 669704 | tf_op jit(solution)/shard_map/ppermute | solution.py:17
  34.3 0.7 copy-start.4
  34.8 2.2 %collective-permute-start.3 = (f32[128,1277]{1,0:T(8,128)S(1)}, f32[128,1277]{1,0:T(8,128)S(1)}, u32[]{:S(2)}, u32[]{:S(2)}) collective-permute-start(f32[128,1277]{1,0:T(8,128)S(1)} %fusion.12), channel_id=1, source_target_pairs={{0,4},{4,0},{8,12},{12,8},{1,5},{5,1},{9,13},{13,9},{2,6},{6,2},{1... | collective-permute-start | bytes 1961480 | tf_op jit(solution)/shard_map/ppermute | solution.py:27
  39.7 21.6 %collective-permute-start.4 = (f32[128,1214]{0,1:T(8,128)}, f32[128,1214]{0,1:T(8,128)S(1)}, u32[]{:S(2)}, u32[]{:S(2)}) collective-permute-start(f32[128,1214]{0,1:T(8,128)} %copy.25), channel_id=1, source_target_pairs={{0,8},{8,0},{4,12},{12,4},{1,9},{9,1},{5,13},{13,5},{2,10},{10,2},... | collective-permute-start | bytes 1864712 | tf_op jit(solution)/shard_map/ppermute | solution.py:27
  57.7 2.4 %copy-start.2 = (f32[4,256,511]{2,1,0:T(8,128)S(1)}, f32[4,256,511]{2,1,0:T(8,128)}, u32[]{:S(2)}) copy-start(f32[4,256,511]{2,1,0:T(8,128)} %reshape.1315) | copy-start | bytes 6279172
  63.6 2.1 %copy-start.3 = (f32[4,256,256]{1,2,0:T(8,128)S(1)}, f32[4,256,256]{1,2,0:T(8,128)}, u32[]{:S(2)}) copy-start(f32[4,256,256]{1,2,0:T(8,128)} %slice_bitcast_fusion) | copy-start | bytes 3145732
  70.7 2.0 %copy-start.1 = (f32[4,128]{1,0:T(4,128)S(1)}, f32[4,128]{1,0:T(4,128)}, u32[]{:S(2)}) copy-start(f32[4,128]{1,0:T(4,128)} %param.6) | copy-start | bytes 6148

commit v5 on v0

--- a/solution.py
+++ b/solution.py
@@ -25,6 +25,15 @@
         if high != low and high < count:
             route += [(low, high), (high, low)]
     return lax.ppermute(block, axis, route)
+
+
+def butterfly_sum(value, axis):
+    count = lax.axis_size(axis)
+    total = value
+    for step in range(1, count):
+        route = [(source, (source + step) % count) for source in range(count)]
+        total = total + lax.ppermute(value, axis, route)
+    return total
 
 
 def shift_rows(upper_rows, offsets, window):
@@ -115,7 +124,9 @@
     chan_rows, time_length = samples.shape
     chan_count = lax.axis_size("chan")
     sample_total = time_length * lax.axis_size("tm")
-    totals, squares = lax.psum((jnp.sum(samples, axis=1), jnp.sum(samples * samples, axis=1)), "tm")
+    totals, squares = butterfly_sum(
+        jnp.stack([jnp.sum(samples, axis=1), jnp.sum(samples * samples, axis=1)]), "tm"
+    )
     average = totals[:, None] / sample_total
     mean_square = squares[:, None] / sample_total
     scaling = lax.rsqrt(mean_square - average * average + epsilon) / math.sqrt(

time: 69.8 us -> 67.3 us (0.964)
  blocking collectives: 13.5 us -> 0 us
  starting transfers between devices: 2.88 us -> 9.04 us
  waiting for transfers between devices: 9.79 us -> 12.7 us
  other arithmetic: 16.7 us -> 18.4 us
    psum x1 -> x0, blocking collectives: 13.5 us -> none  [shards(): lax.psum((jnp.sum(samples, axis=1), jnp.sum(samples * samples, axis=1)),...]
    ppermute x0 -> x3, starting transfers between devices: none -> 6.16 us  [butterfly_sum(): total = total + lax.ppermute(value, axis, route)]
    ppermute x0 -> x3, waiting for transfers between devices: none -> 2.74 us  [butterfly_sum(): total = total + lax.ppermute(value, axis, route)]
    eq x4, other arithmetic: 0.17 us -> 1.94 us  [shift_rows(): chosen = offsets // stride % 2 == 1]
    unnamed x14 -> x12, local copies, waits for them, and re-layouts: 4.4 us -> 4.39 us
  transfers between devices with their start and end apart: 3 -> 6, of which waited for: 3 -> 4; matrix products, arithmetic and copies ran while one was open for 20% -> 23% of each run, Pallas kernels for 0% -> 0%
where the time goes in v5:
time: 67.3 us; the launch traced here: 66.9 us
  local copies, waits for them, and re-layouts  21.8 us (32%)
  other arithmetic  18.4 us (27%)
  waiting for transfers between devices  12.7 us (19%)
  starting transfers between devices  9.04 us (13%)
  matrix products  4.26 us (6%)
    reshape x2, local copies, waits for them, and re-layouts, toeplitz_band(): tiled.reshape(templ_count, block_len, period - 1)[:, :, :block_len]  8.75 us
    select_n x30, other arithmetic, shift_rows(): jnp.where(chosen[:, None], current[:, stride:], current[:, :length])  8.24 us
    ppermute x1, waiting for transfers between devices, from_behind(): lax.ppermute(value, axis, [(source, source + steps) for source in range(l...  6.95 us
    ppermute x3, starting transfers between devices, butterfly_sum(): total = total + lax.ppermute(value, axis, route)  6.16 us
    unnamed x12, local copies, waits for them, and re-layouts  4.39 us
    ppermute x2, waiting for transfers between devices, swapped(): return lax.ppermute(block, axis, route)  3.02 us
    ppermute x3, waiting for transfers between devices, butterfly_sum(): total = total + lax.ppermute(value, axis, route)  2.74 us
    dot_general x1, matrix products, filter_blocks(): jnp.einsum('rni,mit->rmnt', blocks[:, :-1], band_now, precision=lax.Preci...  2.06 us
  transfers between devices with their start and end apart: 6, of which 4 were waited for; matrix products, arithmetic and copies ran while one was open for 23% of the time, Pallas kernels for 0%

profile of v5, /device:TPU:0, one launch (start us, length us, event | category | flops | bytes accessed | tf_op | source)
XLA Modules:
  0.0 66.9 jit_solution(13999174770301231328)
XLA Ops:
  0.0 1.2 %fusion.91 = (f32[128]{0:T(128)S(1)}, f32[128]{0:T(128)S(1)}) fusion(f32[128,1024]{1,0:T(8,128)} %param.4), kind=kLoop, calls=%fused_computation.393 | loop fusion | flops 392960 | bytes 525312 | tf_op jit(solution)/shard_map/reduce_sum | solution.py:128
  1.2 4.1 %collective-permute-start.1 = (f32[2,128]{1,0:T(2,128)S(1)}, f32[2,128]{1,0:T(2,128)S(1)}, u32[]{:S(2)}, u32[]{:S(2)}) collective-permute-start(f32[2,128]{1,0:T(2,128)S(1)} %pad_maximum_fusion.13), channel_id=1, source_target_pairs={{0,2},{1,3},{2,0},{3,1},{4,6},{5,7},{6,4},{7,5},{8,10},{9,11},{10,... | collective-permute-start | bytes 3080 | tf_op jit(solution)/shard_map/ppermute | solution.py:35
  5.3 1.3 %collective-permute-start.2 = (f32[2,128]{1,0:T(2,128)S(1)}, f32[2,128]{1,0:T(2,128)S(1)}, u32[]{:S(2)}, u32[]{:S(2)}) collective-permute-start(f32[2,128]{1,0:T(2,128)S(1)} %pad_maximum_fusion.13), channel_id=1, source_target_pairs={{0,3},{1,0},{2,1},{3,2},{4,7},{5,4},{6,5},{7,6},{8,11},{9,8},{10,9... | collective-permute-start | bytes 3080 | tf_op jit(solution)/shard_map/ppermute | solution.py:35
  6.7 0.7 %collective-permute-start = (f32[2,128]{1,0:T(2,128)S(1)}, f32[2,128]{1,0:T(2,128)S(1)}, u32[]{:S(2)}, u32[]{:S(2)}) collective-permute-start(f32[2,128]{1,0:T(2,128)S(1)} %pad_maximum_fusion.13), channel_id=1, source_target_pairs={{0,1},{1,2},{2,3},{3,0},{4,5},{5,6},{6,7},{7,4},{8,9},{9,10},{10,1... | collective-permute-start | bytes 3080 | tf_op jit(solution)/shard_map/ppermute | solution.py:35
  7.4 1.0 %fusion.46 = (pred[128]{0:T(512)(128)(4,1)S(1)}, pred[128]{0:T(512)(128)(4,1)S(1)}, pred[128]{0:T(512)(128)(4,1)S(1)}, pred[128]{0:T(512)(128)(4,1)S(1)}, pred[1...) fusion(s32[9,128]{1,0:T(8,128)} %param.5), kind=kLoop, calls=%fused_computation.331 | loop fusion | flops 46720 | bytes 6400 | tf_op jit(solution)/shard_map/eq | solution.py:43
  8.3 1.0 %fusion.45 = (pred[128]{0:T(512)(128)(4,1)S(1)}, pred[128]{0:T(512)(128)(4,1)S(1)}, pred[128]{0:T(512)(128)(4,1)S(1)}, pred[128]{0:T(512)(128)(4,1)S(1)}, pred[1...) fusion(s32[9,128]{1,0:T(8,128)} %param.5), kind=kLoop, calls=%fused_computation.330 | loop fusion | flops 51328 | bytes 6016 | tf_op jit(solution)/shard_map/eq | solution.py:43
  9.3 2.7 %collective-permute-done = f32[2,128]{1,0:T(2,128)S(1)} collective-permute-done((f32[2,128]{1,0:T(2,128)S(1)}, f32[2,128]{1,0:T(2,128)S(1)}, u32[]{:S(2)}, u32[]{:S(2)}) %collective-permute-start) | collective-permute-done | bytes 1056 | tf_op jit(solution)/shard_map/ppermute | solution.py:35
  12.1 1.2 %subtract_multiply_fusion = f32[128,1024]{1,0:T(8,128)S(1)} fusion(f32[128,1024]{1,0:T(8,128)} %param.4, f32[128]{0:T(128)S(1)} %fusion.90, f32[128]{0:T(128)S(1)} %multiply_bitcast_fusion), kind=kLoop, calls=%fused_computation.73 | loop fusion | flops 262144 | bytes 1049600 | tf_op jit(solution)/shard_map/mul | solution.py:135
  13.3 1.3 %collective-permute-start.3 = (f32[128,436]{1,0:T(8,128)S(1)}, f32[128,436]{1,0:T(8,128)S(1)}, u32[]{:S(2)}, u32[]{:S(2)}) collective-permute-start(f32[128,436]{1,0:T(8,128)S(1)} %slice.470), channel_id=1, source_target_pairs={{1,0},{2,1},{3,2},{5,4},{6,5},{7,6},{9,8},{10,9},{11,10},{13,12},{... | collective-permute-start | bytes 669704 | tf_op jit(solution)/shard_map/ppermute | solution.py:17
  14.6 7.0 %collective-permute-done.3 = f32[128,436]{1,0:T(8,128)S(1)} collective-permute-done((f32[128,436]{1,0:T(8,128)S(1)}, f32[128,436]{1,0:T(8,128)S(1)}, u32[]{:S(2)}, u32[]{:S(2)}) %collective-permute-start.3) | collective-permute-done | bytes 223264 | tf_op jit(solution)/shard_map/ppermute | solution.py:17
  21.6 0.5 reshape.1316
  22.1 0.6 slice_bitcast_fusion.16
  22.7 0.6 pad_maximum_fusion.1
  23.3 0.5 reshape.1317
  23.9 0.6 pad_maximum_fusion.2
  24.5 0.5 reshape.1318
  25.0 0.3 fusion.4
  25.3 0.5 reshape.1319
  25.9 0.3 pad_maximum_fusion.3
  26.5 0.3 pad_maximum_fusion.4
  27.1 0.3 slice_select_fusion.12
  27.3 0.3 fusion.3
  28.1 0.3 slice_select_fusion.10
  28.4 0.3 slice_select_fusion.9
  28.7 0.3 fusion.2
  29.2 0.3 slice_select_fusion.7
  29.5 0.3 slice_select_fusion.6
  30.1 0.3 fusion.1
  30.6 0.3 slice_select_fusion.3
  30.9 0.3 slice_select_fusion.2
  31.5 0.3 slice_select_fusion
  34.5 0.4 slice_select_fusion.16
  35.9 2.0 %collective-permute-done.4 = f32[128,1277]{1,0:T(8,128)S(1)} collective-permute-done((f32[128,1277]{1,0:T(8,128)S(1)}, f32[128,1277]{1,0:T(8,128)S(1)}, u32[]{:S(2)}, u32[]{:S(2)}) %collective-permute-start.4) | collective-permute-done | bytes 653856 | tf_op jit(solution)/shard_map/ppermute | solution.py:27
  39.6 1.1 %copy.25 = f32[128,1214]{0,1:T(8,128)} copy(f32[128,1214]{1,0:T(8,128)S(1)} %fusion.7) | data formatting | bytes 1243136 | tf_op jit(solution)/shard_map/add | solution.py:67
  40.7 1.5 %collective-permute-start.5 = (f32[128,1214]{0,1:T(8,128)}, f32[128,1214]{0,1:T(8,128)S(1)}, u32[]{:S(2)}, u32[]{:S(2)}) collective-permute-start(f32[128,1214]{0,1:T(8,128)} %copy.25), channel_id=1, source_target_pairs={{0,8},{8,0},{4,12},{12,4},{1,9},{9,1},{5,13},{13,5},{2,10},{10,2},... | collective-permute-start | bytes 1864712 | tf_op jit(solution)/shard_map/ppermute | solution.py:27
  42.2 0.3 fusion.10
  42.5 0.4 broadcast_bitcast_fusion
  42.9 1.4 %copy.42 = f32[1,4,256,512]{3,1,2,0:T(4,128)S(1)} copy(f32[1,4,256,512]{3,2,1,0:T(8,128)S(1)} %get-tuple-element.66) | data formatting | bytes 4194304
  44.3 1.4 %slice.575 = f32[4,130816]{1,0:T(4,128)} slice(f32[4,131072]{1,0:T(4,128)S(1)} %bitcast.377), slice={[0:4], [0:130816]} | slice | bytes 4186112 | tf_op jit(solution)/shard_map/slice | solution.py:96
  45.7 5.1 %reshape.1338 = f32[4,256,511]{2,1,0:T(8,128)} reshape(f32[4,130816]{1,0:T(4,128)} %slice.575) | data formatting | bytes 4186112 | tf_op jit(solution)/shard_map/reshape | solution.py:97
  50.8 1.4 %copy.41 = f32[1,4,256,512]{3,1,2,0:T(4,128)S(1)} copy(f32[1,4,256,512]{3,2,1,0:T(8,128)S(1)} %get-tuple-element.67) | data formatting | bytes 4194304
  52.3 3.6 %reshape.1315 = f32[4,256,511]{2,1,0:T(8,128)} reshape(f32[4,130816]{1,0:T(4,128)S(1)} %slice.468) | data formatting | bytes 4186112 | tf_op jit(solution)/shard_map/reshape | solution.py:97
  56.0 1.0 %collective-permute-done.5 = f32[128,1214]{0,1:T(8,128)S(1)} collective-permute-done((f32[128,1214]{0,1:T(8,128)}, f32[128,1214]{0,1:T(8,128)S(1)}, u32[]{:S(2)}, u32[]{:S(2)}) %collective-permute-start.5) | collective-permute-done | bytes 621600 | tf_op jit(solution)/shard_map/ppermute | solution.py:27
  58.6 1.1 %fusion.9 = f32[128,1151]{1,0:T(8,128)} fusion(f32[128,1183]{1,0:T(8,128)S(1)} %slice_select_fusion.26, f32[128,1214]{1,0:T(8,128)S(1)} %fusion.7, f32[128,1214]{1,0:T(8,128)S(1)} %copy.26, pred[128]{0:T(512)(128)(4,1)S(1)} %get-tuple-element.27, pred[]{:T(512)S(6)} %eq.338), kind=kLoop, calls=%fused_computation.69 | loop fusion | flops 441984 | bytes 2946689 | tf_op jit(solution)/shard_map/add | solution.py:67
  59.6 1.3 %copy.40 = f32[128,1151]{0,1:T(8,128)S(1)} copy(f32[128,1151]{1,0:T(8,128)} %fusion.9) | data formatting | bytes 1178624
  61.0 2.1 %fusion = f32[4,256,128,4]{2,1,3,0:T(8,128)S(1)} fusion(f32[4,256,511]{2,1,0:T(8,128)S(1)} %copy-done.1, f32[128,5,256]{0,2,1:T(8,128)S(1)} %bitcast.382), kind=kOutput, calls=%fused_computation.3 | convolution fusion | flops 1610612736 | bytes 3670016 | tf_op jit(solution)/shard_map/rni,mit->rmnt/dot_general | solution.py:116
  63.1 1.9 %convolution_add_fusion = f32[4,256,128,4]{2,1,3,0:T(8,128)S(1)} fusion(f32[4,256,128,4]{2,1,3,0:T(8,128)S(1)} %fusion, f32[4,256,511]{2,1,0:T(8,128)S(1)} %copy-done.2, f32[128,5,256]{0,2,1:T(8,128)S(1)} %bitcast.383), kind=kOutput, calls=%fused_computation | convolution fusion | flops 1611137024 | bytes 5767168 | tf_op jit(solution)/shard_map/rni,mit->rmnt/dot_general | solution.py:117
  65.0 2.0 %copy.31 = f32[128,4,1024]{2,1,0:T(4,128)} copy(f32[128,4,1024]{0,2,1:T(8,128)S(1)} %bitcast.376) | data formatting | bytes 4194304 | tf_op jit(solution)/shard_map/reshape | solution.py:120
  (71 shorter events, 9.1 us)
Async XLA Ops:
  0.0 42.2 %copy-start = (f32[4,128]{1,0:T(4,128)S(1)}, f32[4,128]{1,0:T(4,128)}, u32[]{:S(2)}) copy-start(f32[4,128]{1,0:T(4,128)} %param.6) | copy-start | bytes 6148
  1.2 8.1 %collective-permute-start.1 = (f32[2,128]{1,0:T(2,128)S(1)}, f32[2,128]{1,0:T(2,128)S(1)}, u32[]{:S(2)}, u32[]{:S(2)}) collective-permute-start(f32[2,128]{1,0:T(2,128)S(1)} %pad_maximum_fusion.13), channel_id=1, source_target_pairs={{0,2},{1,3},{2,0},{3,1},{4,6},{5,7},{6,4},{7,5},{8,10},{9,11},{10,... | collective-permute-start | bytes 3080 | tf_op jit(solution)/shard_map/ppermute | solution.py:35
  5.3 4.0 %collective-permute-start.2 = (f32[2,128]{1,0:T(2,128)S(1)}, f32[2,128]{1,0:T(2,128)S(1)}, u32[]{:S(2)}, u32[]{:S(2)}) collective-permute-start(f32[2,128]{1,0:T(2,128)S(1)} %pad_maximum_fusion.13), channel_id=1, source_target_pairs={{0,3},{1,0},{2,1},{3,2},{4,7},{5,4},{6,5},{7,6},{8,11},{9,8},{10,9... | collective-permute-start | bytes 3080 | tf_op jit(solution)/shard_map/ppermute | solution.py:35
  6.7 5.4 %collective-permute-start = (f32[2,128]{1,0:T(2,128)S(1)}, f32[2,128]{1,0:T(2,128)S(1)}, u32[]{:S(2)}, u32[]{:S(2)}) collective-permute-start(f32[2,128]{1,0:T(2,128)S(1)} %pad_maximum_fusion.13), channel_id=1, source_target_pairs={{0,1},{1,2},{2,3},{3,0},{4,5},{5,6},{6,7},{7,4},{8,9},{9,10},{10,1... | collective-permute-start | bytes 3080 | tf_op jit(solution)/shard_map/ppermute | solution.py:35
  13.3 8.3 %collective-permute-start.3 = (f32[128,436]{1,0:T(8,128)S(1)}, f32[128,436]{1,0:T(8,128)S(1)}, u32[]{:S(2)}, u32[]{:S(2)}) collective-permute-start(f32[128,436]{1,0:T(8,128)S(1)} %slice.470), channel_id=1, source_target_pairs={{1,0},{2,1},{3,2},{5,4},{6,5},{7,6},{9,8},{10,9},{11,10},{13,12},{... | collective-permute-start | bytes 669704 | tf_op jit(solution)/shard_map/ppermute | solution.py:17
  35.8 2.2 %collective-permute-start.4 = (f32[128,1277]{1,0:T(8,128)S(1)}, f32[128,1277]{1,0:T(8,128)S(1)}, u32[]{:S(2)}, u32[]{:S(2)}) collective-permute-start(f32[128,1277]{1,0:T(8,128)S(1)} %fusion.8), channel_id=1, source_target_pairs={{0,4},{4,0},{8,12},{12,8},{1,5},{5,1},{9,13},{13,9},{2,6},{6,2},{1... | collective-permute-start | bytes 1961480 | tf_op jit(solution)/shard_map/ppermute | solution.py:27
  39.3 2.9 %copy-start.3 = (s32[4,128]{1,0:T(4,128)S(1)}, s32[4,128]{1,0:T(4,128)}, u32[]{:S(2)}) copy-start(s32[4,128]{1,0:T(4,128)} %param.7) | copy-start | bytes 6148
  40.7 16.3 %collective-permute-start.5 = (f32[128,1214]{0,1:T(8,128)}, f32[128,1214]{0,1:T(8,128)S(1)}, u32[]{:S(2)}, u32[]{:S(2)}) collective-permute-start(f32[128,1214]{0,1:T(8,128)} %copy.25), channel_id=1, source_target_pairs={{0,8},{8,0},{4,12},{12,4},{1,9},{9,1},{5,13},{13,5},{2,10},{10,2},... | collective-permute-start | bytes 1864712 | tf_op jit(solution)/shard_map/ppermute | solution.py:27
  58.6 2.4 %copy-start.1 = (f32[4,256,511]{2,1,0:T(8,128)S(1)}, f32[4,256,511]{2,1,0:T(8,128)}, u32[]{:S(2)}) copy-start(f32[4,256,511]{2,1,0:T(8,128)} %reshape.1315) | copy-start | bytes 6279172
  61.0 2.1 %copy-start.2 = (f32[4,256,511]{2,1,0:T(8,128)S(1)}, f32[4,256,511]{2,1,0:T(8,128)}, u32[]{:S(2)}) copy-start(f32[4,256,511]{2,1,0:T(8,128)} %reshape.1338) | copy-start | bytes 6279172
